TPU v7x, 32 devices: a whole 2x2x4 slice. The times are simulated.
32 devices in a mesh: dp: 8 (over z, core), tensor: 4 (over y, x).
Axes of the slice: x: 2, y: 2, z: 4, core: 2. Of those that a mesh axis runs over, the one named last changes fastest.
Arguments:
- tokens: bfloat16 [512, 8192], P(None, 'dp'), may hold values from -6 to 6
- w_gate_up: bfloat16 [8192, 2, 28672], P('dp', None, 'tensor'), may hold values from -0.0625 to 0.0625
- w_down: bfloat16 [28672, 8192], P('tensor', 'dp'), may hold values from -0.03125 to 0.03125
- targets: bfloat16 [512, 8192], P(None, 'dp'), may hold values from -3 to 3
- proj_model: bfloat16 [8192, 128], P('dp'), may hold values from -0.0625 to 0.0625
- proj_hidden: bfloat16 [28672, 192], P('tensor'), may hold values from -0.03125 to 0.03125
- store: bfloat16 [4096, 12288], P(('dp', 'tensor')), may hold values from -0.017944336 to 0.017944336
Outputs:
- scores: float32 [4, 4096], P(None, ('dp', 'tensor'))
All inputs are finite; a program needn't handle non-finite values.
Results may differ from a plain program's by a relative error of at most 0.02.
Values may be sent and summed in bfloat16 or wider, within the bound.
No kernel may reach another device: no remote copies, remote signals or barrier semaphores. Data moves between devices by JAX's collectives and lax.ppermute only.
A program may use at most 256 MiB of HBM per device.

v0:
```python
import jax
import jax.numpy as jnp
from jax import lax
from jax.sharding import PartitionSpec as P

RANK = 64
SEQ = 128


def local(tokens, w_gate_up, w_down, targets, proj_model, proj_hidden, store):
    n_data = lax.axis_size("dp")
    total = tokens.shape[0]
    tok_rows = total // n_data
    width_ff = w_down.shape[0]
    hi = lax.Precision.HIGHEST
    tests = total // SEQ
    rows = tokens
    both = jnp.einsum("td,dkf->tkf", rows, w_gate_up, preferred_element_type=jnp.float32)
    gate_up = lax.psum_scatter(
        both.reshape(tok_rows * lax.axis_size("dp"), 2 * width_ff),
        "dp",
        scatter_dimension=0,
        tiled=True,
    )
    gate = gate_up[:, :width_ff]
    up = gate_up[:, width_ff:]
    sig = jax.nn.sigmoid(gate)
    act = gate * sig
    hidden = (act * up).astype(jnp.bfloat16)
    out_part = jnp.dot(
        lax.all_gather(hidden, "dp", axis=0, tiled=True), w_down, preferred_element_type=jnp.float32
    )
    out_full = lax.psum(out_part, "tensor")
    cot = (out_full - targets.astype(jnp.float32)).astype(jnp.bfloat16)
    rows = cot
    grad_hidden = lax.psum_scatter(
        lax.dot_general(
            rows, w_down, (((1,), (1,)), ((), ())), preferred_element_type=jnp.float32
        ).astype(jnp.bfloat16),
        "dp",
        scatter_dimension=0,
        tiled=True,
    ).astype(jnp.float32)
    dgate = (grad_hidden * up * sig * (1.0 + gate * (1.0 - sig))).astype(jnp.bfloat16)
    dup = (grad_hidden * act).astype(jnp.bfloat16)
    side = jnp.concatenate(
        [
            jnp.dot(tokens, proj_model[:, :RANK], preferred_element_type=jnp.float32),
            jnp.dot(cot, proj_model[:, RANK:], preferred_element_type=jnp.float32),
        ],
        axis=1,
    )
    side_sum = lax.psum_scatter(
        side.astype(jnp.bfloat16), "dp", scatter_dimension=0, tiled=True
    ).astype(jnp.float32)
    a_in = side_sum[:, :RANK]
    a_out = side_sum[:, RANK:]
    hid_part = jnp.concatenate(
        [
            jnp.dot(dgate, proj_hidden[:, :RANK], preferred_element_type=jnp.float32),
            jnp.dot(dup, proj_hidden[:, RANK : 2 * RANK], preferred_element_type=jnp.float32),
            jnp.dot(hidden, proj_hidden[:, 2 * RANK :], preferred_element_type=jnp.float32),
        ],
        axis=1,
    )
    position = lax.axis_index("dp") * tok_rows + lax.iota(jnp.int32, tok_rows)
    member = ((position // SEQ)[:, None] == lax.iota(jnp.int32, tests)[None, :]).astype(jnp.float32)
    hid_sum = lax.psum(hid_part.astype(jnp.bfloat16), "tensor").astype(jnp.float32)
    g_gate = jnp.einsum("ts,ti,tj->sij", member, a_in, hid_sum[:, :RANK], precision=hi)
    g_up = jnp.einsum("ts,ti,tj->sij", member, a_in, hid_sum[:, RANK : 2 * RANK], precision=hi)
    g_down = jnp.einsum("ts,ti,tj->sij", member, hid_sum[:, 2 * RANK :], a_out, precision=hi)
    grads = lax.psum(
        jnp.stack([g_gate, g_up, g_down], axis=1).reshape(tests, 3 * RANK * RANK), "dp"
    )
    return lax.dot_general(
        grads.astype(jnp.bfloat16),
        store,
        (((1,), (1,)), ((), ())),
        preferred_element_type=jnp.float32,
    )


def solution(mesh):
    return jax.shard_map(
        local,
        mesh=mesh,
        in_specs=(
            P(None, "dp"),
            P("dp", None, "tensor"),
            P("tensor", "dp"),
            P(None, "dp"),
            P("dp", None),
            P("tensor", None),
            P(("dp", "tensor"), None),
        ),
        out_specs=P(None, ("dp", "tensor")),
        check_vma=False,
    )
```

profile of v0, /device:TPU:0, one launch (start us, length us, event | category | flops | bytes accessed | tf_op | source)
XLA Modules:
  0.0 683.5 jit_solution(1664660564008795075)
XLA Ops:
  6.5 0.0 copy-start
  6.5 0.0 reduce-scatter.6.cloned.1.call-start
  6.5 26.0 %fusion = f32[512,2,7168]{0,2,1:T(8,128)} fusion(bf16[1024,2,7168]{2,1,0:T(2,128)(2,1)} %param.8, bf16[512,1024]{1,0:T(8,128)(2,1)} %param.7), kind=kOutput, calls=%fused_computation | convolution fusion | flops 15032385536 | bytes 59768832 | tf_op jit(solution)/shard_map/td,dkf->tkf/dot_general | solution.py:18
  32.6 29.6 %copy.19 = f32[512,14336]{1,0:T(8,128)} copy(f32[512,14336]{0,1:T(8,128)} %bitcast.36) | data formatting | bytes 58720256 | tf_op jit(solution)/shard_map/reshape | solution.py:20
  62.2 0.0 reduce-scatter.6.cloned.1.call-update
  62.2 0.0 all-gather.2.cloned.1.call-start
  62.2 289.4 %reduce-scatter.6.cloned.1.call-done = f32[64,14336]{1,0:T(8,128)} async-done(((f32[512,14336]{1,0:T(8,128)}), f32[64,14336]{1,0:T(8,128)}) %reduce-scatter.6.cloned.1.call-update) | async-done | bytes 3670032 | tf_op jit(solution)/shard_map/reduce_scatter | solution.py:19
  351.7 3.5 multiply_convert_fusion
  355.1 0.0 all-gather.2.cloned.1.call-update
  355.1 0.0 all-reduce.3.cloned.1.call-start
  355.2 71.9 %all-gather.2.cloned.1.call-done = bf16[512,7168]{1,0:T(8,128)(2,1)} async-done(((bf16[64,7168]{1,0:T(8,128)(2,1)}), bf16[512,7168]{1,0:T(8,128)(2,1)}) %all-gather.2.cloned.1.call-update) | async-done | bytes 7340048 | tf_op jit(solution)/shard_map/all_gather | solution.py:31
  427.0 14.1 %fusion.30 = f32[512,1024]{1,0:T(8,128)} fusion(bf16[512,7168]{1,0:T(8,128)(2,1)} %all-gather.2.cloned.1.call-done, bf16[7168,1024]{1,0:T(8,128)(2,1)} %param.9), kind=kOutput, calls=%fused_computation.53 | convolution fusion | flops 7516192768 | bytes 24117248 | tf_op jit(solution)/shard_map/dot_general | solution.py:30
  441.1 0.0 copy-start.2
  441.1 0.0 all-reduce.3.cloned.1.call-update
  441.1 0.0 reduce-scatter.10.cloned.1.call-start
  441.2 0.9 copy-done.2
  442.1 1.7 convolution_convert_fusion.2
  443.7 65.8 %all-reduce.3.cloned.1.call-done = f32[512,1024]{1,0:T(8,128)} async-done(((f32[512,1024]{1,0:T(8,128)}), f32[512,1024]{1,0:T(8,128)}) %all-reduce.3.cloned.1.call-update) | async-done | bytes 2097168 | tf_op jit(solution)/shard_map/psum | solution.py:33
  509.5 2.4 convolution_convert_fusion.1
  511.9 0.8 copy.24
  512.7 0.0 reduce-scatter.10.cloned.1.call-update
  512.7 0.2 reduce-scatter.8.cloned.1.call-start
  513.0 13.9 %convolution_convert_fusion = bf16[512,7168]{1,0:T(8,128)(2,1)} fusion(bf16[7168,1024]{1,0:T(8,128)(2,1)} %param.9, f32[512,1024]{1,0:T(8,128)} %all-reduce.3.cloned.1.call-done, bf16[512,1024]{1,0:T(8,128)(2,1)} %param.10), kind=kOutput, calls=%fused_computation.2 | convolution fusion | flops 7521435648 | bytes 25165824 | tf_op jit(solution)/shard_map/dot_general | solution.py:37
  526.9 0.0 reduce-scatter.8.cloned.1.call-update
  526.9 1.9 convolution_convert_fusion.3
  528.8 14.2 %reduce-scatter.10.cloned.1.call-done = bf16[64,128]{1,0:T(8,128)(2,1)} async-done(((bf16[512,128]{1,0:T(8,128)(2,1)}), bf16[64,128]{1,0:T(8,128)(2,1)}) %reduce-scatter.10.cloned.1.call-update) | async-done | bytes 16400 | tf_op jit(solution)/shard_map/reduce_scatter | solution.py:53
  543.0 0.8 copy.26
  543.8 79.3 %reduce-scatter.8.cloned.1.call-done = bf16[64,7168]{1,0:T(8,128)(2,1)} async-done(((bf16[512,7168]{1,0:T(8,128)(2,1)}), bf16[64,7168]{1,0:T(8,128)(2,1)}) %reduce-scatter.8.cloned.1.call-update) | async-done | bytes 917520 | tf_op jit(solution)/shard_map/reduce_scatter | solution.py:36
  623.1 0.0 copy-start.1
  623.1 0.0 copy-start.4
  623.1 3.5 convolution_convert_fusion.5
  626.6 0.1 copy-done.1
  626.8 0.2 copy-done.4
  627.0 0.0 copy-start.3
  627.0 1.9 convolution_convert_fusion.4
  628.9 0.1 pad_maximum_fusion.2
  629.0 16.2 %psum.22 = bf16[64,192]{1,0:T(8,128)(2,1)S(1)} all-reduce(bf16[64,192]{1,0:T(8,128)(2,1)S(1)} %pad_maximum_fusion.2), channel_id=1, replica_groups=mesh['dp'=8,'tensor'=4] {'tensor'}, use_global_device_ids=true, to_apply=%region_4.5 | all-reduce | flops 12288 | bytes 49152 | tf_op jit(solution)/shard_map/psum | solution.py:68
  645.2 0.2 convolution_bitcast_fusion.2
  645.4 0.3 convolution_bitcast_fusion.1
  645.7 0.1 copy.20
  645.8 0.0 copy-done.3
  645.8 0.3 convolution_bitcast_fusion
  646.1 0.8 reshape.26
  647.0 28.5 %all-reduce.4 = bf16[4,12288]{1,0:T(4,128)(2,1)S(1)} all-reduce(f32[4,12288]{1,0:T(4,128)} %reshape.26), channel_id=1, replica_groups=mesh['dp'=8,'tensor'=4] {'dp'}, use_global_device_ids=true, to_apply=%region_5.6 | all-reduce | flops 49152 | bytes 294912 | tf_op jit(solution)/shard_map/psum | solution.py:72
  675.5 0.0 copy-done
  675.5 1.5 fusion.31
  (7 shorter events, 0.1 us)
Async XLA Ops:
  6.5 669.0 %copy-start = (bf16[128,12288]{1,0:T(8,128)(2,1)S(1)}, bf16[128,12288]{1,0:T(8,128)(2,1)}, u32[]{:S(2)}) copy-start(bf16[128,12288]{1,0:T(8,128)(2,1)} %param.13) | copy-start | bytes 9437188
  6.5 345.1 %reduce-scatter.6.cloned.1.call-start = ((), (), s32[]{:S(2)}) async-start(), calls=%async_computation.3 | async-start | bytes 33030144 | tf_op jit(solution)/shard_map/reduce_scatter | solution.py:19
  62.2 364.9 %all-gather.2.cloned.1.call-start = ((), (), s32[]{:S(2)}) async-start(), calls=%async_computation.4 | async-start | bytes 8257536 | tf_op jit(solution)/shard_map/all_gather | solution.py:31
  355.1 154.4 %all-reduce.3.cloned.1.call-start = ((), (), s32[]{:S(2)}) async-start(), calls=%async_computation.5 | async-start | bytes 4194304 | tf_op jit(solution)/shard_map/psum | solution.py:33
  441.1 0.9 copy-start.2
  441.1 101.9 %reduce-scatter.10.cloned.1.call-start = ((), (), s32[]{:S(2)}) async-start(), calls=%async_computation.7 | async-start | bytes 147456 | tf_op jit(solution)/shard_map/reduce_scatter | solution.py:53
  512.7 110.3 %reduce-scatter.8.cloned.1.call-start = ((), (), s32[]{:S(2)}) async-start(), calls=%async_computation.6 | async-start | bytes 8257536 | tf_op jit(solution)/shard_map/reduce_scatter | solution.py:36
  623.1 3.7 copy-start.1
  623.1 3.9 copy-start.4
  627.0 18.8 %copy-start.3 = (bf16[64,128]{1,0:T(8,128)(2,1)S(1)}, bf16[64,128]{1,0:T(8,128)(2,1)}, u32[]{:S(2)}) copy-start(bf16[64,128]{1,0:T(8,128)(2,1)} %reduce-scatter.10.cloned.1.call-done) | copy-start | bytes 49156
Sparse Core Ops, SparseCore 0:
  62.3 289.3 reduce-scatter.5
  355.3 71.7 all-gather.1
  441.3 68.2 all-reduce.2
  512.8 30.1 reduce-scatter.9
  545.2 77.8 reduce-scatter.7
where the time goes:
time: 684 us
  waiting for transfers between devices  521 us (76%)
  matrix products  67.5 us (10%)
  blocking collectives  44.7 us (7%)
  local copies, waits for them, and re-layouts  33.4 us (5%)
  between operations  13.3 us (2%)
    reduce_scatter x1, waiting for transfers between devices, local(): lax.psum_scatter(both.reshape(tok_rows * lax.axis_size('dp'), 2 * width_f...  289 us
    reduce_scatter x1, waiting for transfers between devices, local(): lax.psum_scatter(lax.dot_general(rows, w_down, (((1,), (1,)), ((), ())),...  79.3 us
    all_gather x1, waiting for transfers between devices, local(): lax.all_gather(hidden, 'dp', axis=0, tiled=True)  71.9 us
    psum x1, waiting for transfers between devices, local(): out_full = lax.psum(out_part, 'tensor')  65.8 us
    reshape x1, local copies, waits for them, and re-layouts, local(): both.reshape(tok_rows * lax.axis_size('dp'), 2 * width_ff)  29.6 us
    psum x1, blocking collectives, local(): lax.psum(jnp.stack([g_gate, g_up, g_down], axis=1).reshape(tests, 3 * RAN...  28.5 us
    dot_general x1, matrix products, local(): jnp.einsum('td,dkf->tkf', rows, w_gate_up, preferred_element_type=jnp.flo...  26 us
    psum x1, blocking collectives, local(): lax.psum(hid_part.astype(jnp.bfloat16), 'tensor').astype(jnp.float32)  16.2 us
  transfers between devices with their start and end apart: 5, of which 5 were waited for; matrix products, arithmetic and copies ran while one was open for 3% of the time, Pallas kernels for 0%

commit v1 on v0

v1 whole, which is shorter than its diff:
```python
import jax
import jax.numpy as jnp
import numpy as np
from jax import lax
from jax.sharding import Mesh, PartitionSpec as P

RANK = 64
SEQ = 128
CHUNKS = 8


def reduce_to_ends(part, n_z, chunks):
    z = lax.axis_index("z")
    half = part.shape[0] // 2
    rows = half // chunks
    low, high = part[:half], part[half:]
    left = [(i, i - 1) for i in range(1, n_z)]
    right = [(i, i + 1) for i in range(n_z - 1)]
    recv_l = jnp.zeros((rows,) + part.shape[1:], jnp.bfloat16)
    recv_r = recv_l
    outs_l, outs_r = [], []
    for step in range(chunks + n_z - 1):
        k_l = jnp.clip(step - (n_z - 1 - z), 0, chunks - 1)
        k_r = jnp.clip(step - z, 0, chunks - 1)
        acc_l = lax.dynamic_slice_in_dim(low, k_l * rows, rows, 0) + recv_l.astype(jnp.float32)
        acc_r = lax.dynamic_slice_in_dim(high, k_r * rows, rows, 0) + recv_r.astype(jnp.float32)
        if step >= n_z - 1:
            outs_l.append(acc_l)
            outs_r.append(acc_r)
        if step < chunks + n_z - 2:
            recv_l = lax.ppermute(acc_l.astype(jnp.bfloat16), "z", left)
            recv_r = lax.ppermute(acc_r.astype(jnp.bfloat16), "z", right)
    return jnp.concatenate(outs_l, axis=0), jnp.concatenate(outs_r, axis=0)


def bcast_from_ends(low_own, high_own, n_z, chunks):
    z = lax.axis_index("z")
    half = low_own.shape[0]
    rows = half // chunks
    left = [(i, i - 1) for i in range(1, n_z)]
    right = [(i, i + 1) for i in range(n_z - 1)]
    recv_l = jnp.zeros((rows,) + low_own.shape[1:], low_own.dtype)
    recv_r = recv_l
    got_l, got_r = [], []
    for step in range(chunks + n_z - 2):
        k = jnp.clip(step, 0, chunks - 1)
        send_l = jnp.where(z == 0, lax.dynamic_slice_in_dim(low_own, k * rows, rows, 0), recv_l)
        send_r = jnp.where(z == n_z - 1, lax.dynamic_slice_in_dim(high_own, k * rows, rows, 0), recv_r)
        recv_l = lax.ppermute(send_l, "z", right)
        recv_r = lax.ppermute(send_r, "z", left)
        got_l.append(recv_l)
        got_r.append(recv_r)
    got_l = jnp.stack(got_l)
    got_r = jnp.stack(got_r)
    start_l = jnp.clip(z - 1, 0, n_z - 2)
    start_r = jnp.clip(n_z - 2 - z, 0, n_z - 2)
    low = lax.dynamic_slice_in_dim(got_l, start_l, chunks, 0).reshape(low_own.shape)
    high = lax.dynamic_slice_in_dim(got_r, start_r, chunks, 0).reshape(high_own.shape)
    low = jnp.where(z == 0, low_own, low)
    high = jnp.where(z == n_z - 1, high_own, high)
    return jnp.concatenate([low, high], axis=0)


def local(tokens, w_gate_up, w_down, targets, proj_model, proj_hidden, store):
    n_z = lax.axis_size("z")
    n_core = lax.axis_size("core")
    z = lax.axis_index("z")
    core = lax.axis_index("core")
    total = tokens.shape[0]
    half = total // 2
    width_ff = w_down.shape[0]
    width_h = width_ff // n_core
    hi = lax.Precision.HIGHEST
    tests = total // SEQ
    chunks = CHUNKS

    a_in_part = jnp.dot(tokens, proj_model[:, :RANK], preferred_element_type=jnp.float32)

    both = jnp.einsum("td,dkf->tkf", tokens, w_gate_up, preferred_element_type=jnp.float32)
    both = both.reshape(total, 2, n_core, width_h)
    both = lax.psum_scatter(both, "core", scatter_dimension=2, tiled=False)
    low, high = reduce_to_ends(both, n_z, chunks)

    def act_of(gu):
        gate = gu[:, 0]
        up = gu[:, 1]
        sig = jax.nn.sigmoid(gate)
        act = gate * sig
        return gate, up, sig, act, (act * up).astype(jnp.bfloat16)

    g_l, u_l, s_l, a_l, h_l = act_of(low)
    g_h, u_h, s_h, a_h, h_h = act_of(high)

    hidden_half = bcast_from_ends(h_l, h_h, n_z, chunks)
    hidden = lax.all_gather(hidden_half, "core", axis=1, tiled=True)
    out_part = jnp.dot(hidden, w_down, preferred_element_type=jnp.float32)
    out_full = lax.psum(out_part, "tensor")
    cot = (out_full - targets.astype(jnp.float32)).astype(jnp.bfloat16)

    a_out_part = jnp.dot(cot, proj_model[:, RANK:], preferred_element_type=jnp.float32)
    side = lax.psum(jnp.concatenate([a_in_part, a_out_part], axis=1), ("z", "core"))

    dh_part = lax.dot_general(cot, w_down, (((1,), (1,)), ((), ())), preferred_element_type=jnp.float32)
    dh_part = lax.psum_scatter(dh_part.reshape(total, n_core, width_h), "core", scatter_dimension=1, tiled=False)
    dh_l, dh_h = reduce_to_ends(dh_part, n_z, chunks)

    ph = lax.dynamic_slice_in_dim(proj_hidden, core * width_h, width_h, 0)

    def b_of(dh, gate, up, sig, act, hid):
        dgate = (dh * up * sig * (1.0 + gate * (1.0 - sig))).astype(jnp.bfloat16)
        dup = (dh * act).astype(jnp.bfloat16)
        return jnp.concatenate(
            [
                jnp.dot(dgate, ph[:, :RANK], preferred_element_type=jnp.float32),
                jnp.dot(dup, ph[:, RANK : 2 * RANK], preferred_element_type=jnp.float32),
                jnp.dot(hid, ph[:, 2 * RANK :], preferred_element_type=jnp.float32),
            ],
            axis=1,
        )

    b_l = b_of(dh_l, g_l, u_l, s_l, a_l, h_l)
    b_h = b_of(dh_h, g_h, u_h, s_h, a_h, h_h)
    is_low = z == 0
    is_high = z == n_z - 1
    b_mine = jnp.where(is_low, b_l, b_h)
    b_mine = lax.psum(b_mine, ("core", "tensor"))
    side_mine = lax.dynamic_slice_in_dim(side, jnp.where(is_low, 0, half), half, 0)
    a_in = side_mine[:, :RANK]
    a_out = side_mine[:, RANK:]
    ht = half // SEQ
    position = lax.iota(jnp.int32, half)
    member = ((position // SEQ)[:, None] == lax.iota(jnp.int32, ht)[None, :]).astype(jnp.float32)
    g_gate = jnp.einsum("ts,ti,tj->sij", member, a_in, b_mine[:, :RANK], precision=hi)
    g_up = jnp.einsum("ts,ti,tj->sij", member, a_in, b_mine[:, RANK : 2 * RANK], precision=hi)
    g_down = jnp.einsum("ts,ti,tj->sij", member, b_mine[:, 2 * RANK :], a_out, precision=hi)
    g_half = jnp.stack([g_gate, g_up, g_down], axis=1).reshape(ht, 3 * RANK * RANK)
    zeros = jnp.zeros_like(g_half)
    g_low = jnp.where(is_low, g_half, zeros)
    g_high = jnp.where(jnp.logical_and(is_high, jnp.logical_not(is_low)), g_half, zeros)
    grads = lax.psum(jnp.concatenate([g_low, g_high], axis=0), "z")
    return lax.dot_general(
        grads.astype(jnp.bfloat16),
        store,
        (((1,), (1,)), ((), ())),
        preferred_element_type=jnp.float32,
    )


def solution(mesh):
    n_dp = mesh.shape["dp"]
    n_t = mesh.shape["tensor"]
    devices = np.asarray(mesh.devices).reshape(n_dp // 2, 2, n_t)
    fine = Mesh(devices, ("z", "core", "tensor"))
    dp = ("z", "core")
    return jax.shard_map(
        local,
        mesh=fine,
        in_specs=(
            P(None, dp),
            P(dp, None, "tensor"),
            P("tensor", dp),
            P(None, dp),
            P(dp, None),
            P("tensor", None),
            P(dp + ("tensor",), None),
        ),
        out_specs=P(None, dp + ("tensor",)),
        check_vma=False,
    )
```

time: 684 us -> 697 us (1.019); the launches traced: 684 us -> 686 us
  waiting for transfers between devices: 521 us -> 328 us
  starting transfers between devices: 0.35 us -> 173 us
  blocking collectives: 44.7 us -> 22.4 us
  local copies, waits for them, and re-layouts: 33.4 us -> 55.4 us
  other arithmetic: 3.62 us -> 18.3 us
    reduce_scatter x3 -> x2, waiting for transfers between devices: 383 us -> 58.6 us  [the longest x1 43 us: local(): both = lax.psum_scatter(both, 'core', scatter_dimension=2, tiled=False)]
    ppermute x0 -> x60, starting transfers between devices: none -> 173 us  [the longest x20 90.1 us: reduce_to_ends(): recv_r = lax.ppermute(acc_r.astype(jnp.bfloat16), 'z', right)]
    ppermute x0 -> x60, waiting for transfers between devices: none -> 125 us  [the longest x20 64.1 us: reduce_to_ends(): recv_r = lax.ppermute(acc_r.astype(jnp.bfloat16), 'z', right)]
    psum x0 -> x2, waiting for transfers between devices: none -> 53.5 us  [the longest x1 53.4 us: local(): b_mine = lax.psum(b_mine, ('core', 'tensor'))]
    all_gather x1, waiting for transfers between devices: 71.9 us -> 19.8 us  [local(): hidden = lax.all_gather(hidden_half, 'core', axis=1, tiled=True)]
    psum x2 -> x1, blocking collectives: 44.7 us -> 22.4 us  [local(): grads = lax.psum(jnp.concatenate([g_low, g_high], axis=0), 'z')]
    slice x0 -> x4, local copies, waits for them, and re-layouts: none -> 16.6 us  [the longest x2 14.9 us: reduce_to_ends(): low, high = (part[:half], part[half:])]
    dot_general x9 -> x12, matrix products: 62 us -> 69.8 us  [the longest x1 27.8 us: local(): jnp.einsum('td,dkf->tkf', tokens, w_gate_up, preferred_element_type=jnp.f...]
  transfers between devices with their start and end apart: 5 -> 66, of which waited for: 5 -> 49; matrix products, arithmetic and copies ran while one was open for 3% -> 5% of each run, Pallas kernels for 0% -> 0%
where the time goes in v1:
time: 697 us; the launch traced here: 686 us
  waiting for transfers between devices  328 us (47%)
  starting transfers between devices  173 us (25%)
  matrix products  73.9 us (11%)
  local copies, waits for them, and re-layouts  55.4 us (8%)
  blocking collectives  22.4 us (3%)
  other arithmetic  18.3 us (3%)
  between operations  15.4 us (2%)
    ppermute x20, starting transfers between devices, reduce_to_ends(): recv_r = lax.ppermute(acc_r.astype(jnp.bfloat16), 'z', right)  90.1 us
    psum x1, waiting for transfers between devices, local(): out_full = lax.psum(out_part, 'tensor')  70.7 us
    ppermute x20, waiting for transfers between devices, reduce_to_ends(): recv_r = lax.ppermute(acc_r.astype(jnp.bfloat16), 'z', right)  64.1 us
    psum x1, waiting for transfers between devices, local(): b_mine = lax.psum(b_mine, ('core', 'tensor'))  53.4 us
    ppermute x10, starting transfers between devices, bcast_from_ends(): recv_l = lax.ppermute(send_l, 'z', right)  43.7 us
    reduce_scatter x1, waiting for transfers between devices, local(): both = lax.psum_scatter(both, 'core', scatter_dimension=2, tiled=False)  43 us
    ppermute x20, waiting for transfers between devices, reduce_to_ends(): recv_l = lax.ppermute(acc_l.astype(jnp.bfloat16), 'z', left)  33.6 us
    dot_general x1, matrix products, local(): jnp.einsum('td,dkf->tkf', tokens, w_gate_up, preferred_element_type=jnp.f...  27.8 us
  transfers between devices with their start and end apart: 66, of which 49 were waited for; matrix products, arithmetic and copies ran while one was open for 5% of the time, Pallas kernels for 0%

profile of v1, /device:TPU:0, one launch (start us, length us, event | category | flops | bytes accessed | tf_op | source)
XLA Modules:
  0.0 686.4 jit_solution(12924978306551481694)
XLA Ops:
  6.5 27.8 %fusion = f32[512,2,7168]{2,0,1:T(8,128)} fusion(bf16[1024,2,7168]{2,1,0:T(2,128)(2,1)} %param.8, bf16[512,1024]{1,0:T(8,128)(2,1)} %param.7), kind=kOutput, calls=%fused_computation.1 | convolution fusion | flops 15032385536 | bytes 59768832 | tf_op jit(solution)/shard_map/td,dkf->tkf/dot_general | solution.py:79
  34.3 22.2 %copy.22 = f32[2,64,2,8,3584]{4,3,1,0,2:T(8,128)} copy(f32[2,64,2,8,3584]{4,3,2,1,0:T(8,128)} %bitcast.364) | data formatting | bytes 58720256 | tf_op jit(solution)/shard_map/reshape | solution.py:80
  56.7 43.0 %reduce-scatter.3.cloned.1.call-done = f32[512,2,1,3584]{3,0,1,2:T(8,128)} async-done(((f32[512,2,2,3584]{3,0,1,2:T(8,128)}), f32[512,2,1,3584]{3,0,1,2:T(8,128)}) %reduce-scatter.3.cloned.1.call-update) | async-done | bytes 14680080 | tf_op jit(solution)/shard_map/reduce_scatter | solution.py:81
  99.7 11.3 %fusion.115 = (f32[256,2,1,3584]{3,0,1,2:T(8,128)}, f32[256,2,1,3584]{3,0,1,2:T(8,128)}) fusion(f32[512,2,1,3584]{3,0,1,2:T(8,128)} %reduce-scatter.3.cloned.1.call-done), kind=kLoop, calls=%fused_computation.233 | loop fusion | bytes 29360128 | tf_op jit(solution)/shard_map/slice | solution.py:16
  112.4 3.9 collective-permute-start.20
  118.9 7.7 %collective-permute-done.20 = bf16[32,2,3584]{2,0,1:T(8,128)(2,1)S(1)} collective-permute-done((bf16[32,2,3584]{2,0,1:T(8,128)(2,1)S(1)}, bf16[32,2,3584]{2,0,1:T(8,128)(2,1)S(1)}, u32[]{:S(2)}, u32[]{:S(2)}) %collective-permute-start.20) | collective-permute-done | bytes 458784 | tf_op jit(solution)/shard_map/ppermute | solution.py:32
  127.8 4.4 collective-permute-start.21
  134.8 6.8 collective-permute-done.21
  142.9 4.7 collective-permute-start.22
  149.0 7.1 %collective-permute-done.22 = bf16[32,2,3584]{2,0,1:T(8,128)(2,1)S(1)} collective-permute-done((bf16[32,2,3584]{2,0,1:T(8,128)(2,1)S(1)}, bf16[32,2,3584]{2,0,1:T(8,128)(2,1)S(1)}, u32[]{:S(2)}, u32[]{:S(2)}) %collective-permute-start.22) | collective-permute-done | bytes 458784 | tf_op jit(solution)/shard_map/ppermute | solution.py:32
  157.4 4.4 collective-permute-start.23
  163.3 6.1 collective-permute-done.23
  169.6 4.4 collective-permute-start.24
  175.4 5.2 collective-permute-done.24
  180.8 4.4 collective-permute-start.25
  186.6 5.1 collective-permute-done.25
  191.9 4.4 collective-permute-start.26
  197.7 6.2 collective-permute-done.26
  204.1 4.4 collective-permute-start.27
  209.9 7.3 %collective-permute-done.27 = bf16[32,2,3584]{2,0,1:T(8,128)(2,1)S(1)} collective-permute-done((bf16[32,2,3584]{2,0,1:T(8,128)(2,1)S(1)}, bf16[32,2,3584]{2,0,1:T(8,128)(2,1)S(1)}, u32[]{:S(2)}, u32[]{:S(2)}) %collective-permute-start.27) | collective-permute-done | bytes 458784 | tf_op jit(solution)/shard_map/ppermute | solution.py:32
  217.4 4.4 collective-permute-start.28
  223.2 8.1 %collective-permute-done.28 = bf16[32,2,3584]{2,0,1:T(8,128)(2,1)S(1)} collective-permute-done((bf16[32,2,3584]{2,0,1:T(8,128)(2,1)S(1)}, bf16[32,2,3584]{2,0,1:T(8,128)(2,1)S(1)}, u32[]{:S(2)}, u32[]{:S(2)}) %collective-permute-start.28) | collective-permute-done | bytes 458784 | tf_op jit(solution)/shard_map/ppermute | solution.py:32
  231.4 4.4 collective-permute-start.29
  237.8 4.0 collective-permute-done.29
  248.0 3.6 collective-permute-start.10
  255.1 4.4 collective-permute-start.11
  263.0 4.6 collective-permute-start.12
  269.1 2.9 collective-permute-done.12
  272.1 4.8 collective-permute-start.13
  278.3 4.3 collective-permute-done.13
  282.6 4.4 collective-permute-start.14
  288.6 3.8 collective-permute-done.14
  292.4 4.4 collective-permute-start.15
  298.7 2.8 collective-permute-done.15
  301.5 4.4 collective-permute-start.16
  309.7 4.4 collective-permute-start.17
  317.6 4.4 collective-permute-start.18
  325.6 4.4 collective-permute-start.19
  337.3 19.8 %all-gather.2.cloned.1.call-done = bf16[512,7168]{1,0:T(8,128)(2,1)} async-done(((bf16[512,3584]{1,0:T(8,128)(2,1)}), bf16[512,7168]{1,0:T(8,128)(2,1)}) %all-gather.2.cloned.1.call-update) | async-done | bytes 7340048 | tf_op jit(solution)/shard_map/all_gather | solution.py:95
  357.1 14.1 %fusion.117 = f32[512,1024]{1,0:T(8,128)} fusion(bf16[512,7168]{1,0:T(8,128)(2,1)} %all-gather.2.cloned.1.call-done, bf16[7168,1024]{1,0:T(8,128)(2,1)} %param.9), kind=kOutput, calls=%fused_computation.235 | convolution fusion | flops 7516192768 | bytes 24117248 | tf_op jit(solution)/shard_map/dot_general | solution.py:96
  371.4 70.7 %all-reduce.5.cloned.1.call-done = f32[512,1024]{1,0:T(8,128)} async-done(((f32[512,1024]{1,0:T(8,128)}), f32[512,1024]{1,0:T(8,128)}) %all-reduce.5.cloned.1.call-update) | async-done | bytes 2097168 | tf_op jit(solution)/shard_map/psum | solution.py:97
  442.1 15.0 %fusion.114 = f32[512,7168]{1,0:T(8,128)} fusion(bf16[7168,1024]{1,0:T(8,128)(2,1)} %param.9, f32[512,1024]{1,0:T(8,128)} %all-reduce.5.cloned.1.call-done, bf16[512,1024]{1,0:T(8,128)(2,1)} %param.10), kind=kOutput, calls=%fused_computation.232 | convolution fusion | flops 7517765632 | bytes 32505856 | tf_op jit(solution)/shard_map/dot_general | solution.py:103
  457.1 11.5 %copy.23 = f32[64,2,8,3584]{3,2,0,1:T(8,128)} copy(f32[64,2,8,3584]{3,2,1,0:T(8,128)} %bitcast.365) | data formatting | bytes 29360128 | tf_op jit(solution)/shard_map/reshape | solution.py:104
  477.1 15.6 %reduce-scatter.5.cloned.1.call-done = f32[512,1,3584]{2,0,1:T(8,128)} async-done(((f32[512,2,3584]{2,0,1:T(8,128)}), f32[512,1,3584]{2,0,1:T(8,128)}) %reduce-scatter.5.cloned.1.call-update) | async-done | bytes 7340048 | tf_op jit(solution)/shard_map/reduce_scatter | solution.py:104
  492.7 3.6 fusion.116
  497.7 4.6 collective-permute-start.50
  502.3 4.2 collective-permute-done.40
  507.9 4.5 collective-permute-start.51
  512.5 3.8 collective-permute-done.41
  517.7 4.6 collective-permute-start.52
  526.1 4.6 collective-permute-start.53
  534.5 4.4 collective-permute-start.54
  538.9 2.4 collective-permute-done.44
  542.7 4.8 collective-permute-start.55
  547.5 3.0 collective-permute-done.45
  552.0 4.6 collective-permute-start.56
  556.6 4.1 collective-permute-done.46
  562.1 4.8 collective-permute-start.57
  566.9 3.5 collective-permute-done.47
  571.9 4.5 collective-permute-start.58
  576.4 3.6 collective-permute-done.48
  581.7 4.8 collective-permute-start.59
  595.6 53.4 %all-reduce.9.cloned.1.call-done = f32[256,192]{0,1:T(8,128)} async-done(((f32[256,192]{0,1:T(8,128)}), f32[256,192]{0,1:T(8,128)}) %all-reduce.9.cloned.1.call-update) | async-done | bytes 196624 | tf_op jit(solution)/shard_map/psum | solution.py:126
  655.2 22.4 %all-reduce.10 = bf16[4,12288]{1,0:T(4,128)(2,1)S(1)} all-reduce(f32[4,12288]{1,0:T(4,128)S(1)} %pad_maximum_fusion.3), channel_id=1, replica_groups=mesh['z'=4,'core'=2,'tensor'=4] {'z'}, use_global_device_ids=true, to_apply=%region_5.6 | all-reduce | flops 49152 | bytes 294912 | tf_op jit(solution)/shard_map/psum | solution.py:140
  (231 shorter events, 104.8 us)
Async XLA Ops:
  6.5 93.2 %reduce-scatter.3.cloned.1.call-start = ((), (), s32[]{:S(2)}) async-start(), calls=%async_computation.2 | async-start | bytes 44040192 | tf_op jit(solution)/shard_map/reduce_scatter | solution.py:81
  56.6 300.5 %all-gather.2.cloned.1.call-start = ((), (), s32[]{:S(2)}) async-start(), calls=%async_computation.3 | async-start | bytes 11010048 | tf_op jit(solution)/shard_map/all_gather | solution.py:95
  112.4 14.2 %collective-permute-start.20 = (bf16[32,2,3584]{2,0,1:T(8,128)(2,1)S(1)}, bf16[32,2,3584]{2,0,1:T(8,128)(2,1)S(1)}, u32[]{:S(2)}, u32[]{:S(2)}) collective-permute-start(bf16[32,2,3584]{2,0,1:T(8,128)(2,1)S(1)} %fusion.44), channel_id=1, source_target_pairs={{0,8},{8,16},{16,24},{1,9},{9,17},{17,25},{2,10},{10,18},{18,26},{... | collective-permute-start | bytes 1376264 | tf_op jit(solution)/shard_map/ppermute | solution.py:32
  117.6 14.7 %collective-permute-start = (bf16[32,2,3584]{2,0,1:T(8,128)(2,1)S(1)}, bf16[32,2,3584]{2,0,1:T(8,128)(2,1)S(1)}, u32[]{:S(2)}, u32[]{:S(2)}) collective-permute-start(bf16[32,2,3584]{2,0,1:T(8,128)(2,1)S(1)} %fusion.43), channel_id=1, source_target_pairs={{8,0},{16,8},{24,16},{9,1},{17,9},{25,17},{10,2},{18,10},{26,18},{... | collective-permute-start | bytes 1376264 | tf_op jit(solution)/shard_map/ppermute | solution.py:31
  127.8 13.9 %collective-permute-start.21 = (bf16[32,2,3584]{2,0,1:T(8,128)(2,1)S(1)}, bf16[32,2,3584]{2,0,1:T(8,128)(2,1)S(1)}, u32[]{:S(2)}, u32[]{:S(2)}) collective-permute-start(bf16[32,2,3584]{2,0,1:T(8,128)(2,1)S(1)} %fusion.10), channel_id=1, source_target_pairs={{0,8},{8,16},{16,24},{1,9},{9,17},{17,25},{2,10},{10,18},{18,26},{... | collective-permute-start | bytes 1376264 | tf_op jit(solution)/shard_map/ppermute | solution.py:32
  133.5 14.1 %collective-permute-start.1 = (bf16[32,2,3584]{2,0,1:T(8,128)(2,1)S(1)}, bf16[32,2,3584]{2,0,1:T(8,128)(2,1)S(1)}, u32[]{:S(2)}, u32[]{:S(2)}) collective-permute-start(bf16[32,2,3584]{2,0,1:T(8,128)(2,1)S(1)} %fusion.13), channel_id=1, source_target_pairs={{8,0},{16,8},{24,16},{9,1},{17,9},{25,17},{10,2},{18,10},{26,18},{... | collective-permute-start | bytes 1376264 | tf_op jit(solution)/shard_map/ppermute | solution.py:31
  142.9 13.2 %collective-permute-start.22 = (bf16[32,2,3584]{2,0,1:T(8,128)(2,1)S(1)}, bf16[32,2,3584]{2,0,1:T(8,128)(2,1)S(1)}, u32[]{:S(2)}, u32[]{:S(2)}) collective-permute-start(bf16[32,2,3584]{2,0,1:T(8,128)(2,1)S(1)} %fusion.11), channel_id=1, source_target_pairs={{0,8},{8,16},{16,24},{1,9},{9,17},{17,25},{2,10},{10,18},{18,26},{... | collective-permute-start | bytes 1376264 | tf_op jit(solution)/shard_map/ppermute | solution.py:32
  147.7 14.1 %collective-permute-start.2 = (bf16[32,2,3584]{2,0,1:T(8,128)(2,1)S(1)}, bf16[32,2,3584]{2,0,1:T(8,128)(2,1)S(1)}, u32[]{:S(2)}, u32[]{:S(2)}) collective-permute-start(bf16[32,2,3584]{2,0,1:T(8,128)(2,1)S(1)} %fusion.14), channel_id=1, source_target_pairs={{8,0},{16,8},{24,16},{9,1},{17,9},{25,17},{10,2},{18,10},{26,18},{... | collective-permute-start | bytes 1376264 | tf_op jit(solution)/shard_map/ppermute | solution.py:31
  157.4 12.0 %collective-permute-start.23 = (bf16[32,2,3584]{2,0,1:T(8,128)(2,1)S(1)}, bf16[32,2,3584]{2,0,1:T(8,128)(2,1)S(1)}, u32[]{:S(2)}, u32[]{:S(2)}) collective-permute-start(bf16[32,2,3584]{2,0,1:T(8,128)(2,1)S(1)} %get-tuple-element.33), channel_id=1, source_target_pairs={{0,8},{8,16},{16,24},{1,9},{9,17},{17,25},{2,10},{10,18},{18,26},{... | collective-permute-start | bytes 1376264 | tf_op jit(solution)/shard_map/ppermute | solution.py:32
  162.0 12.0 %collective-permute-start.3 = (bf16[32,2,3584]{2,0,1:T(8,128)(2,1)S(1)}, bf16[32,2,3584]{2,0,1:T(8,128)(2,1)S(1)}, u32[]{:S(2)}, u32[]{:S(2)}) collective-permute-start(bf16[32,2,3584]{2,0,1:T(8,128)(2,1)S(1)} %get-tuple-element.19), channel_id=1, source_target_pairs={{8,0},{16,8},{24,16},{9,1},{17,9},{25,17},{10,2},{18,10},{26,18},{... | collective-permute-start | bytes 1376264 | tf_op jit(solution)/shard_map/ppermute | solution.py:31
  169.6 11.1 %collective-permute-start.24 = (bf16[32,2,3584]{2,0,1:T(8,128)(2,1)S(1)}, bf16[32,2,3584]{2,0,1:T(8,128)(2,1)S(1)}, u32[]{:S(2)}, u32[]{:S(2)}) collective-permute-start(bf16[32,2,3584]{2,0,1:T(8,128)(2,1)S(1)} %get-tuple-element.31), channel_id=1, source_target_pairs={{0,8},{8,16},{16,24},{1,9},{9,17},{17,25},{2,10},{10,18},{18,26},{... | collective-permute-start | bytes 1376264 | tf_op jit(solution)/shard_map/ppermute | solution.py:32
  174.1 11.1 %collective-permute-start.4 = (bf16[32,2,3584]{2,0,1:T(8,128)(2,1)S(1)}, bf16[32,2,3584]{2,0,1:T(8,128)(2,1)S(1)}, u32[]{:S(2)}, u32[]{:S(2)}) collective-permute-start(bf16[32,2,3584]{2,0,1:T(8,128)(2,1)S(1)} %get-tuple-element.17), channel_id=1, source_target_pairs={{8,0},{16,8},{24,16},{9,1},{17,9},{25,17},{10,2},{18,10},{26,18},{... | collective-permute-start | bytes 1376264 | tf_op jit(solution)/shard_map/ppermute | solution.py:31
  180.8 11.0 %collective-permute-start.25 = (bf16[32,2,3584]{2,0,1:T(8,128)(2,1)S(1)}, bf16[32,2,3584]{2,0,1:T(8,128)(2,1)S(1)}, u32[]{:S(2)}, u32[]{:S(2)}) collective-permute-start(bf16[32,2,3584]{2,0,1:T(8,128)(2,1)S(1)} %get-tuple-element.29), channel_id=1, source_target_pairs={{0,8},{8,16},{16,24},{1,9},{9,17},{17,25},{2,10},{10,18},{18,26},{... | collective-permute-start | bytes 1376264 | tf_op jit(solution)/shard_map/ppermute | solution.py:32
  185.3 11.0 %collective-permute-start.5 = (bf16[32,2,3584]{2,0,1:T(8,128)(2,1)S(1)}, bf16[32,2,3584]{2,0,1:T(8,128)(2,1)S(1)}, u32[]{:S(2)}, u32[]{:S(2)}) collective-permute-start(bf16[32,2,3584]{2,0,1:T(8,128)(2,1)S(1)} %get-tuple-element.15), channel_id=1, source_target_pairs={{8,0},{16,8},{24,16},{9,1},{17,9},{25,17},{10,2},{18,10},{26,18},{... | collective-permute-start | bytes 1376264 | tf_op jit(solution)/shard_map/ppermute | solution.py:31
  191.9 12.1 %collective-permute-start.26 = (bf16[32,2,3584]{2,0,1:T(8,128)(2,1)S(1)}, bf16[32,2,3584]{2,0,1:T(8,128)(2,1)S(1)}, u32[]{:S(2)}, u32[]{:S(2)}) collective-permute-start(bf16[32,2,3584]{2,0,1:T(8,128)(2,1)S(1)} %get-tuple-element.27), channel_id=1, source_target_pairs={{0,8},{8,16},{16,24},{1,9},{9,17},{17,25},{2,10},{10,18},{18,26},{... | collective-permute-start | bytes 1376264 | tf_op jit(solution)/shard_map/ppermute | solution.py:32
  196.4 12.1 %collective-permute-start.6 = (bf16[32,2,3584]{2,0,1:T(8,128)(2,1)S(1)}, bf16[32,2,3584]{2,0,1:T(8,128)(2,1)S(1)}, u32[]{:S(2)}, u32[]{:S(2)}) collective-permute-start(bf16[32,2,3584]{2,0,1:T(8,128)(2,1)S(1)} %get-tuple-element.13), channel_id=1, source_target_pairs={{8,0},{16,8},{24,16},{9,1},{17,9},{25,17},{10,2},{18,10},{26,18},{... | collective-permute-start | bytes 1376264 | tf_op jit(solution)/shard_map/ppermute | solution.py:31
  204.1 13.2 %collective-permute-start.27 = (bf16[32,2,3584]{2,0,1:T(8,128)(2,1)S(1)}, bf16[32,2,3584]{2,0,1:T(8,128)(2,1)S(1)}, u32[]{:S(2)}, u32[]{:S(2)}) collective-permute-start(bf16[32,2,3584]{2,0,1:T(8,128)(2,1)S(1)} %get-tuple-element.25), channel_id=1, source_target_pairs={{0,8},{8,16},{16,24},{1,9},{9,17},{17,25},{2,10},{10,18},{18,26},{... | collective-permute-start | bytes 1376264 | tf_op jit(solution)/shard_map/ppermute | solution.py:32
  208.6 13.2 %collective-permute-start.7 = (bf16[32,2,3584]{2,0,1:T(8,128)(2,1)S(1)}, bf16[32,2,3584]{2,0,1:T(8,128)(2,1)S(1)}, u32[]{:S(2)}, u32[]{:S(2)}) collective-permute-start(bf16[32,2,3584]{2,0,1:T(8,128)(2,1)S(1)} %get-tuple-element.11), channel_id=1, source_target_pairs={{8,0},{16,8},{24,16},{9,1},{17,9},{25,17},{10,2},{18,10},{26,18},{... | collective-permute-start | bytes 1376264 | tf_op jit(solution)/shard_map/ppermute | solution.py:31
  217.4 14.0 %collective-permute-start.28 = (bf16[32,2,3584]{2,0,1:T(8,128)(2,1)S(1)}, bf16[32,2,3584]{2,0,1:T(8,128)(2,1)S(1)}, u32[]{:S(2)}, u32[]{:S(2)}) collective-permute-start(bf16[32,2,3584]{2,0,1:T(8,128)(2,1)S(1)} %get-tuple-element.23), channel_id=1, source_target_pairs={{0,8},{8,16},{16,24},{1,9},{9,17},{17,25},{2,10},{10,18},{18,26},{... | collective-permute-start | bytes 1376264 | tf_op jit(solution)/shard_map/ppermute | solution.py:32
  221.9 14.3 %collective-permute-start.8 = (bf16[32,2,3584]{2,0,1:T(8,128)(2,1)S(1)}, bf16[32,2,3584]{2,0,1:T(8,128)(2,1)S(1)}, u32[]{:S(2)}, u32[]{:S(2)}) collective-permute-start(bf16[32,2,3584]{2,0,1:T(8,128)(2,1)S(1)} %get-tuple-element.9), channel_id=1, source_target_pairs={{8,0},{16,8},{24,16},{9,1},{17,9},{25,17},{10,2},{18,10},{26,18},{... | collective-permute-start | bytes 1376264 | tf_op jit(solution)/shard_map/ppermute | solution.py:31
  231.4 10.4 %collective-permute-start.29 = (bf16[32,2,3584]{2,0,1:T(8,128)(2,1)S(1)}, bf16[32,2,3584]{2,0,1:T(8,128)(2,1)S(1)}, u32[]{:S(2)}, u32[]{:S(2)}) collective-permute-start(bf16[32,2,3584]{2,0,1:T(8,128)(2,1)S(1)} %get-tuple-element.21), channel_id=1, source_target_pairs={{0,8},{8,16},{16,24},{1,9},{9,17},{17,25},{2,10},{10,18},{18,26},{... | collective-permute-start | bytes 1376264 | tf_op jit(solution)/shard_map/ppermute | solution.py:32
  236.3 10.4 %collective-permute-start.9 = (bf16[32,2,3584]{2,0,1:T(8,128)(2,1)S(1)}, bf16[32,2,3584]{2,0,1:T(8,128)(2,1)S(1)}, u32[]{:S(2)}, u32[]{:S(2)}) collective-permute-start(bf16[32,2,3584]{2,0,1:T(8,128)(2,1)S(1)} %get-tuple-element.7), channel_id=1, source_target_pairs={{8,0},{16,8},{24,16},{9,1},{17,9},{25,17},{10,2},{18,10},{26,18},{... | collective-permute-start | bytes 1376264 | tf_op jit(solution)/shard_map/ppermute | solution.py:31
  243.1 8.8 %collective-permute-start.30 = (bf16[32,3584]{1,0:T(8,128)(2,1)S(1)}, bf16[32,3584]{1,0:T(8,128)(2,1)S(1)}, u32[]{:S(2)}, u32[]{:S(2)}) collective-permute-start(bf16[32,3584]{1,0:T(8,128)(2,1)S(1)} %slice_select_fusion.6), channel_id=1, source_target_pairs={{8,0},{16,8},{24,16},{9,1},{17,9},{25,17},{10,2},{18,10},{26,18},{... | collective-permute-start | bytes 688136 | tf_op jit(solution)/shard_map/ppermute | solution.py:50
  251.9 7.9 %collective-permute-start.31 = (bf16[32,3584]{1,0:T(8,128)(2,1)S(1)}, bf16[32,3584]{1,0:T(8,128)(2,1)S(1)}, u32[]{:S(2)}, u32[]{:S(2)}) collective-permute-start(bf16[32,3584]{1,0:T(8,128)(2,1)S(1)} %slice_select_fusion.5), channel_id=1, source_target_pairs={{8,0},{16,8},{24,16},{9,1},{17,9},{25,17},{10,2},{18,10},{26,18},{... | collective-permute-start | bytes 688136 | tf_op jit(solution)/shard_map/ppermute | solution.py:50
  255.1 7.9 %collective-permute-start.11 = (bf16[32,3584]{1,0:T(8,128)(2,1)S(1)}, bf16[32,3584]{1,0:T(8,128)(2,1)S(1)}, u32[]{:S(2)}, u32[]{:S(2)}) collective-permute-start(bf16[32,3584]{1,0:T(8,128)(2,1)S(1)} %slice_select_fusion.12), channel_id=1, source_target_pairs={{0,8},{8,16},{16,24},{1,9},{9,17},{17,25},{2,10},{10,18},{18,26},{... | collective-permute-start | bytes 688136 | tf_op jit(solution)/shard_map/ppermute | solution.py:49
  259.9 7.9 %collective-permute-start.32 = (bf16[32,3584]{1,0:T(8,128)(2,1)S(1)}, bf16[32,3584]{1,0:T(8,128)(2,1)S(1)}, u32[]{:S(2)}, u32[]{:S(2)}) collective-permute-start(bf16[32,3584]{1,0:T(8,128)(2,1)S(1)} %slice_select_fusion.4), channel_id=1, source_target_pairs={{8,0},{16,8},{24,16},{9,1},{17,9},{25,17},{10,2},{18,10},{26,18},{... | collective-permute-start | bytes 688136 | tf_op jit(solution)/shard_map/ppermute | solution.py:50
  263.0 9.0 %collective-permute-start.12 = (bf16[32,3584]{1,0:T(8,128)(2,1)S(1)}, bf16[32,3584]{1,0:T(8,128)(2,1)S(1)}, u32[]{:S(2)}, u32[]{:S(2)}) collective-permute-start(bf16[32,3584]{1,0:T(8,128)(2,1)S(1)} %slice_select_fusion.11), channel_id=1, source_target_pairs={{0,8},{8,16},{16,24},{1,9},{9,17},{17,25},{2,10},{10,18},{18,26},{... | collective-permute-start | bytes 688136 | tf_op jit(solution)/shard_map/ppermute | solution.py:49
  267.8 9.1 %collective-permute-start.33 = (bf16[32,3584]{1,0:T(8,128)(2,1)S(1)}, bf16[32,3584]{1,0:T(8,128)(2,1)S(1)}, u32[]{:S(2)}, u32[]{:S(2)}) collective-permute-start(bf16[32,3584]{1,0:T(8,128)(2,1)S(1)} %slice_select_fusion.3), channel_id=1, source_target_pairs={{8,0},{16,8},{24,16},{9,1},{17,9},{25,17},{10,2},{18,10},{26,18},{... | collective-permute-start | bytes 688136 | tf_op jit(solution)/shard_map/ppermute | solution.py:50
  272.1 10.4 %collective-permute-start.13 = (bf16[32,3584]{1,0:T(8,128)(2,1)S(1)}, bf16[32,3584]{1,0:T(8,128)(2,1)S(1)}, u32[]{:S(2)}, u32[]{:S(2)}) collective-permute-start(bf16[32,3584]{1,0:T(8,128)(2,1)S(1)} %slice_select_fusion.10), channel_id=1, source_target_pairs={{0,8},{8,16},{16,24},{1,9},{9,17},{17,25},{2,10},{10,18},{18,26},{... | collective-permute-start | bytes 688136 | tf_op jit(solution)/shard_map/ppermute | solution.py:49
  277.0 10.3 %collective-permute-start.34 = (bf16[32,3584]{1,0:T(8,128)(2,1)S(1)}, bf16[32,3584]{1,0:T(8,128)(2,1)S(1)}, u32[]{:S(2)}, u32[]{:S(2)}) collective-permute-start(bf16[32,3584]{1,0:T(8,128)(2,1)S(1)} %slice_select_fusion.2), channel_id=1, source_target_pairs={{8,0},{16,8},{24,16},{9,1},{17,9},{25,17},{10,2},{18,10},{26,18},{... | collective-permute-start | bytes 688136 | tf_op jit(solution)/shard_map/ppermute | solution.py:50
  282.6 9.8 %collective-permute-start.14 = (bf16[32,3584]{1,0:T(8,128)(2,1)S(1)}, bf16[32,3584]{1,0:T(8,128)(2,1)S(1)}, u32[]{:S(2)}, u32[]{:S(2)}) collective-permute-start(bf16[32,3584]{1,0:T(8,128)(2,1)S(1)} %slice_select_fusion.9), channel_id=1, source_target_pairs={{0,8},{8,16},{16,24},{1,9},{9,17},{17,25},{2,10},{10,18},{18,26},{... | collective-permute-start | bytes 688136 | tf_op jit(solution)/shard_map/ppermute | solution.py:49
  287.3 10.1 %collective-permute-start.35 = (bf16[32,3584]{1,0:T(8,128)(2,1)S(1)}, bf16[32,3584]{1,0:T(8,128)(2,1)S(1)}, u32[]{:S(2)}, u32[]{:S(2)}) collective-permute-start(bf16[32,3584]{1,0:T(8,128)(2,1)S(1)} %slice_select_fusion.1), channel_id=1, source_target_pairs={{8,0},{16,8},{24,16},{9,1},{17,9},{25,17},{10,2},{18,10},{26,18},{... | collective-permute-start | bytes 688136 | tf_op jit(solution)/shard_map/ppermute | solution.py:50
  292.4 9.0 %collective-permute-start.15 = (bf16[32,3584]{1,0:T(8,128)(2,1)S(1)}, bf16[32,3584]{1,0:T(8,128)(2,1)S(1)}, u32[]{:S(2)}, u32[]{:S(2)}) collective-permute-start(bf16[32,3584]{1,0:T(8,128)(2,1)S(1)} %slice_select_fusion.8), channel_id=1, source_target_pairs={{0,8},{8,16},{16,24},{1,9},{9,17},{17,25},{2,10},{10,18},{18,26},{... | collective-permute-start | bytes 688136 | tf_op jit(solution)/shard_map/ppermute | solution.py:49
  297.4 9.0 %collective-permute-start.36 = (bf16[32,3584]{1,0:T(8,128)(2,1)S(1)}, bf16[32,3584]{1,0:T(8,128)(2,1)S(1)}, u32[]{:S(2)}, u32[]{:S(2)}) collective-permute-start(bf16[32,3584]{1,0:T(8,128)(2,1)S(1)} %slice_select_fusion), channel_id=1, source_target_pairs={{8,0},{16,8},{24,16},{9,1},{17,9},{25,17},{10,2},{18,10},{26,18},{... | collective-permute-start | bytes 688136 | tf_op jit(solution)/shard_map/ppermute | solution.py:50
  301.5 8.1 %collective-permute-start.16 = (bf16[32,3584]{1,0:T(8,128)(2,1)S(1)}, bf16[32,3584]{1,0:T(8,128)(2,1)S(1)}, u32[]{:S(2)}, u32[]{:S(2)}) collective-permute-start(bf16[32,3584]{1,0:T(8,128)(2,1)S(1)} %slice_select_fusion.7), channel_id=1, source_target_pairs={{0,8},{8,16},{16,24},{1,9},{9,17},{17,25},{2,10},{10,18},{18,26},{... | collective-permute-start | bytes 688136 | tf_op jit(solution)/shard_map/ppermute | solution.py:49
  306.5 8.2 %collective-permute-start.37 = (bf16[32,3584]{1,0:T(8,128)(2,1)S(1)}, bf16[32,3584]{1,0:T(8,128)(2,1)S(1)}, u32[]{:S(2)}, u32[]{:S(2)}) collective-permute-start(bf16[32,3584]{1,0:T(8,128)(2,1)S(1)} %broadcast_select_fusion.2), channel_id=1, source_target_pairs={{8,0},{16,8},{24,16},{9,1},{17,9},{25,17},{10,2},{18,10},{26,18},{... | collective-permute-start | bytes 688136 | tf_op jit(solution)/shard_map/ppermute | solution.py:50
  309.7 7.9 %collective-permute-start.17 = (bf16[32,3584]{1,0:T(8,128)(2,1)S(1)}, bf16[32,3584]{1,0:T(8,128)(2,1)S(1)}, u32[]{:S(2)}, u32[]{:S(2)}) collective-permute-start(bf16[32,3584]{1,0:T(8,128)(2,1)S(1)} %broadcast_select_fusion.5), channel_id=1, source_target_pairs={{0,8},{8,16},{16,24},{1,9},{9,17},{17,25},{2,10},{10,18},{18,26},{... | collective-permute-start | bytes 688136 | tf_op jit(solution)/shard_map/ppermute | solution.py:49
  314.6 7.9 %collective-permute-start.38 = (bf16[32,3584]{1,0:T(8,128)(2,1)S(1)}, bf16[32,3584]{1,0:T(8,128)(2,1)S(1)}, u32[]{:S(2)}, u32[]{:S(2)}) collective-permute-start(bf16[32,3584]{1,0:T(8,128)(2,1)S(1)} %broadcast_select_fusion.1), channel_id=1, source_target_pairs={{8,0},{16,8},{24,16},{9,1},{17,9},{25,17},{10,2},{18,10},{26,18},{... | collective-permute-start | bytes 688136 | tf_op jit(solution)/shard_map/ppermute | solution.py:50
  317.6 7.9 %collective-permute-start.18 = (bf16[32,3584]{1,0:T(8,128)(2,1)S(1)}, bf16[32,3584]{1,0:T(8,128)(2,1)S(1)}, u32[]{:S(2)}, u32[]{:S(2)}) collective-permute-start(bf16[32,3584]{1,0:T(8,128)(2,1)S(1)} %broadcast_select_fusion.4), channel_id=1, source_target_pairs={{0,8},{8,16},{16,24},{1,9},{9,17},{17,25},{2,10},{10,18},{18,26},{... | collective-permute-start | bytes 688136 | tf_op jit(solution)/shard_map/ppermute | solution.py:49
  325.6 7.9 %collective-permute-start.19 = (bf16[32,3584]{1,0:T(8,128)(2,1)S(1)}, bf16[32,3584]{1,0:T(8,128)(2,1)S(1)}, u32[]{:S(2)}, u32[]{:S(2)}) collective-permute-start(bf16[32,3584]{1,0:T(8,128)(2,1)S(1)} %broadcast_select_fusion.3), channel_id=1, source_target_pairs={{0,8},{8,16},{16,24},{1,9},{9,17},{17,25},{2,10},{10,18},{18,26},{... | collective-permute-start | bytes 688136 | tf_op jit(solution)/shard_map/ppermute | solution.py:49
  337.3 104.9 %all-reduce.5.cloned.1.call-start = ((), (), s32[]{:S(2)}) async-start(), calls=%async_computation.4 | async-start | bytes 4194304 | tf_op jit(solution)/shard_map/psum | solution.py:97
  371.2 121.5 %reduce-scatter.5.cloned.1.call-start = ((), (), s32[]{:S(2)}) async-start(), calls=%async_computation.6 | async-start | bytes 22020096 | tf_op jit(solution)/shard_map/reduce_scatter | solution.py:104
  468.6 126.1 %all-reduce.7.cloned.1.call-start = ((), (), s32[]{:S(2)}) async-start(), calls=%async_computation.5 | async-start | bytes 524288 | tf_op jit(solution)/shard_map/psum | solution.py:101
  477.0 172.0 %all-reduce.9.cloned.1.call-start = ((), (), s32[]{:S(2)}) async-start(), calls=%async_computation.7 | async-start | bytes 393216 | tf_op jit(solution)/shard_map/psum | solution.py:126
  496.4 10.1 %collective-permute-start.40 = (bf16[32,3584]{1,0:T(8,128)(2,1)S(1)}, bf16[32,3584]{1,0:T(8,128)(2,1)S(1)}, u32[]{:S(2)}, u32[]{:S(2)}) collective-permute-start(bf16[32,3584]{1,0:T(8,128)(2,1)S(1)} %fusion.93), channel_id=1, source_target_pairs={{8,0},{16,8},{24,16},{9,1},{17,9},{25,17},{10,2},{18,10},{26,18},{... | collective-permute-start | bytes 688136 | tf_op jit(solution)/shard_map/ppermute | solution.py:31
  497.7 10.2 %collective-permute-start.50 = (bf16[32,3584]{1,0:T(8,128)(2,1)S(1)}, bf16[32,3584]{1,0:T(8,128)(2,1)S(1)}, u32[]{:S(2)}, u32[]{:S(2)}) collective-permute-start(bf16[32,3584]{1,0:T(8,128)(2,1)S(1)} %fusion.94), channel_id=1, source_target_pairs={{0,8},{8,16},{16,24},{1,9},{9,17},{17,25},{2,10},{10,18},{18,26},{... | collective-permute-start | bytes 688136 | tf_op jit(solution)/shard_map/ppermute | solution.py:32
  506.6 9.7 %collective-permute-start.41 = (bf16[32,3584]{1,0:T(8,128)(2,1)S(1)}, bf16[32,3584]{1,0:T(8,128)(2,1)S(1)}, u32[]{:S(2)}, u32[]{:S(2)}) collective-permute-start(bf16[32,3584]{1,0:T(8,128)(2,1)S(1)} %fusion.49), channel_id=1, source_target_pairs={{8,0},{16,8},{24,16},{9,1},{17,9},{25,17},{10,2},{18,10},{26,18},{... | collective-permute-start | bytes 688136 | tf_op jit(solution)/shard_map/ppermute | solution.py:31
  507.9 9.6 %collective-permute-start.51 = (bf16[32,3584]{1,0:T(8,128)(2,1)S(1)}, bf16[32,3584]{1,0:T(8,128)(2,1)S(1)}, u32[]{:S(2)}, u32[]{:S(2)}) collective-permute-start(bf16[32,3584]{1,0:T(8,128)(2,1)S(1)} %fusion.46), channel_id=1, source_target_pairs={{0,8},{8,16},{16,24},{1,9},{9,17},{17,25},{2,10},{10,18},{18,26},{... | collective-permute-start | bytes 688136 | tf_op jit(solution)/shard_map/ppermute | solution.py:32
  516.3 8.3 %collective-permute-start.42 = (bf16[32,3584]{1,0:T(8,128)(2,1)S(1)}, bf16[32,3584]{1,0:T(8,128)(2,1)S(1)}, u32[]{:S(2)}, u32[]{:S(2)}) collective-permute-start(bf16[32,3584]{1,0:T(8,128)(2,1)S(1)} %fusion.50), channel_id=1, source_target_pairs={{8,0},{16,8},{24,16},{9,1},{17,9},{25,17},{10,2},{18,10},{26,18},{... | collective-permute-start | bytes 688136 | tf_op jit(solution)/shard_map/ppermute | solution.py:31
  517.7 8.3 %collective-permute-start.52 = (bf16[32,3584]{1,0:T(8,128)(2,1)S(1)}, bf16[32,3584]{1,0:T(8,128)(2,1)S(1)}, u32[]{:S(2)}, u32[]{:S(2)}) collective-permute-start(bf16[32,3584]{1,0:T(8,128)(2,1)S(1)} %fusion.47), channel_id=1, source_target_pairs={{0,8},{8,16},{16,24},{1,9},{9,17},{17,25},{2,10},{10,18},{18,26},{... | collective-permute-start | bytes 688136 | tf_op jit(solution)/shard_map/ppermute | solution.py:32
  524.7 8.1 %collective-permute-start.43 = (bf16[32,3584]{1,0:T(8,128)(2,1)S(1)}, bf16[32,3584]{1,0:T(8,128)(2,1)S(1)}, u32[]{:S(2)}, u32[]{:S(2)}) collective-permute-start(bf16[32,3584]{1,0:T(8,128)(2,1)S(1)} %get-tuple-element.63), channel_id=1, source_target_pairs={{8,0},{16,8},{24,16},{9,1},{17,9},{25,17},{10,2},{18,10},{26,18},{... | collective-permute-start | bytes 688136 | tf_op jit(solution)/shard_map/ppermute | solution.py:31
  526.1 8.3 %collective-permute-start.53 = (bf16[32,3584]{1,0:T(8,128)(2,1)S(1)}, bf16[32,3584]{1,0:T(8,128)(2,1)S(1)}, u32[]{:S(2)}, u32[]{:S(2)}) collective-permute-start(bf16[32,3584]{1,0:T(8,128)(2,1)S(1)} %get-tuple-element.49), channel_id=1, source_target_pairs={{0,8},{8,16},{16,24},{1,9},{9,17},{17,25},{2,10},{10,18},{18,26},{... | collective-permute-start | bytes 688136 | tf_op jit(solution)/shard_map/ppermute | solution.py:32
  532.9 8.4 %collective-permute-start.44 = (bf16[32,3584]{1,0:T(8,128)(2,1)S(1)}, bf16[32,3584]{1,0:T(8,128)(2,1)S(1)}, u32[]{:S(2)}, u32[]{:S(2)}) collective-permute-start(bf16[32,3584]{1,0:T(8,128)(2,1)S(1)} %get-tuple-element.61), channel_id=1, source_target_pairs={{8,0},{16,8},{24,16},{9,1},{17,9},{25,17},{10,2},{18,10},{26,18},{... | collective-permute-start | bytes 688136 | tf_op jit(solution)/shard_map/ppermute | solution.py:31
  534.5 8.2 %collective-permute-start.54 = (bf16[32,3584]{1,0:T(8,128)(2,1)S(1)}, bf16[32,3584]{1,0:T(8,128)(2,1)S(1)}, u32[]{:S(2)}, u32[]{:S(2)}) collective-permute-start(bf16[32,3584]{1,0:T(8,128)(2,1)S(1)} %get-tuple-element.47), channel_id=1, source_target_pairs={{0,8},{8,16},{16,24},{1,9},{9,17},{17,25},{2,10},{10,18},{18,26},{... | collective-permute-start | bytes 688136 | tf_op jit(solution)/shard_map/ppermute | solution.py:32
  541.3 9.2 %collective-permute-start.45 = (bf16[32,3584]{1,0:T(8,128)(2,1)S(1)}, bf16[32,3584]{1,0:T(8,128)(2,1)S(1)}, u32[]{:S(2)}, u32[]{:S(2)}) collective-permute-start(bf16[32,3584]{1,0:T(8,128)(2,1)S(1)} %get-tuple-element.59), channel_id=1, source_target_pairs={{8,0},{16,8},{24,16},{9,1},{17,9},{25,17},{10,2},{18,10},{26,18},{... | collective-permute-start | bytes 688136 | tf_op jit(solution)/shard_map/ppermute | solution.py:31
  542.7 9.2 %collective-permute-start.55 = (bf16[32,3584]{1,0:T(8,128)(2,1)S(1)}, bf16[32,3584]{1,0:T(8,128)(2,1)S(1)}, u32[]{:S(2)}, u32[]{:S(2)}) collective-permute-start(bf16[32,3584]{1,0:T(8,128)(2,1)S(1)} %get-tuple-element.45), channel_id=1, source_target_pairs={{0,8},{8,16},{16,24},{1,9},{9,17},{17,25},{2,10},{10,18},{18,26},{... | collective-permute-start | bytes 688136 | tf_op jit(solution)/shard_map/ppermute | solution.py:32
  550.6 10.0 %collective-permute-start.46 = (bf16[32,3584]{1,0:T(8,128)(2,1)S(1)}, bf16[32,3584]{1,0:T(8,128)(2,1)S(1)}, u32[]{:S(2)}, u32[]{:S(2)}) collective-permute-start(bf16[32,3584]{1,0:T(8,128)(2,1)S(1)} %get-tuple-element.57), channel_id=1, source_target_pairs={{8,0},{16,8},{24,16},{9,1},{17,9},{25,17},{10,2},{18,10},{26,18},{... | collective-permute-start | bytes 688136 | tf_op jit(solution)/shard_map/ppermute | solution.py:31
  552.0 10.0 %collective-permute-start.56 = (bf16[32,3584]{1,0:T(8,128)(2,1)S(1)}, bf16[32,3584]{1,0:T(8,128)(2,1)S(1)}, u32[]{:S(2)}, u32[]{:S(2)}) collective-permute-start(bf16[32,3584]{1,0:T(8,128)(2,1)S(1)} %get-tuple-element.43), channel_id=1, source_target_pairs={{0,8},{8,16},{16,24},{1,9},{9,17},{17,25},{2,10},{10,18},{18,26},{... | collective-permute-start | bytes 688136 | tf_op jit(solution)/shard_map/ppermute | solution.py:32
  560.7 9.7 %collective-permute-start.47 = (bf16[32,3584]{1,0:T(8,128)(2,1)S(1)}, bf16[32,3584]{1,0:T(8,128)(2,1)S(1)}, u32[]{:S(2)}, u32[]{:S(2)}) collective-permute-start(bf16[32,3584]{1,0:T(8,128)(2,1)S(1)} %get-tuple-element.55), channel_id=1, source_target_pairs={{8,0},{16,8},{24,16},{9,1},{17,9},{25,17},{10,2},{18,10},{26,18},{... | collective-permute-start | bytes 688136 | tf_op jit(solution)/shard_map/ppermute | solution.py:31
  562.1 9.7 %collective-permute-start.57 = (bf16[32,3584]{1,0:T(8,128)(2,1)S(1)}, bf16[32,3584]{1,0:T(8,128)(2,1)S(1)}, u32[]{:S(2)}, u32[]{:S(2)}) collective-permute-start(bf16[32,3584]{1,0:T(8,128)(2,1)S(1)} %get-tuple-element.41), channel_id=1, source_target_pairs={{0,8},{8,16},{16,24},{1,9},{9,17},{17,25},{2,10},{10,18},{18,26},{... | collective-permute-start | bytes 688136 | tf_op jit(solution)/shard_map/ppermute | solution.py:32
  570.4 9.6 %collective-permute-start.48 = (bf16[32,3584]{1,0:T(8,128)(2,1)S(1)}, bf16[32,3584]{1,0:T(8,128)(2,1)S(1)}, u32[]{:S(2)}, u32[]{:S(2)}) collective-permute-start(bf16[32,3584]{1,0:T(8,128)(2,1)S(1)} %get-tuple-element.53), channel_id=1, source_target_pairs={{8,0},{16,8},{24,16},{9,1},{17,9},{25,17},{10,2},{18,10},{26,18},{... | collective-permute-start | bytes 688136 | tf_op jit(solution)/shard_map/ppermute | solution.py:31
  571.9 9.8 %collective-permute-start.58 = (bf16[32,3584]{1,0:T(8,128)(2,1)S(1)}, bf16[32,3584]{1,0:T(8,128)(2,1)S(1)}, u32[]{:S(2)}, u32[]{:S(2)}) collective-permute-start(bf16[32,3584]{1,0:T(8,128)(2,1)S(1)} %get-tuple-element.39), channel_id=1, source_target_pairs={{0,8},{8,16},{16,24},{1,9},{9,17},{17,25},{2,10},{10,18},{18,26},{... | collective-permute-start | bytes 688136 | tf_op jit(solution)/shard_map/ppermute | solution.py:32
  580.1 8.2 %collective-permute-start.49 = (bf16[32,3584]{1,0:T(8,128)(2,1)S(1)}, bf16[32,3584]{1,0:T(8,128)(2,1)S(1)}, u32[]{:S(2)}, u32[]{:S(2)}) collective-permute-start(bf16[32,3584]{1,0:T(8,128)(2,1)S(1)} %get-tuple-element.51), channel_id=1, source_target_pairs={{8,0},{16,8},{24,16},{9,1},{17,9},{25,17},{10,2},{18,10},{26,18},{... | collective-permute-start | bytes 688136 | tf_op jit(solution)/shard_map/ppermute | solution.py:31
  581.7 9.5 %collective-permute-start.59 = (bf16[32,3584]{1,0:T(8,128)(2,1)S(1)}, bf16[32,3584]{1,0:T(8,128)(2,1)S(1)}, u32[]{:S(2)}, u32[]{:S(2)}) collective-permute-start(bf16[32,3584]{1,0:T(8,128)(2,1)S(1)} %get-tuple-element.37), channel_id=1, source_target_pairs={{0,8},{8,16},{16,24},{1,9},{9,17},{17,25},{2,10},{10,18},{18,26},{... | collective-permute-start | bytes 688136 | tf_op jit(solution)/shard_map/ppermute | solution.py:32
  (18 other events, 1214.5 us)
Sparse Core Ops, SparseCore 0:
  56.7 42.9 reduce-scatter.2
  337.4 19.6 all-gather.1
  371.3 70.7 all-reduce.4
  468.8 23.8 reduce-scatter.4
  495.0 57.1 all-reduce.6
  594.9 54.1 all-reduce.8

commit v2 on v0

v2 whole, which is shorter than its diff:
```python
import jax
import jax.numpy as jnp
import numpy as np
from jax import lax
from jax.sharding import Mesh, PartitionSpec as P

RANK = 64
SEQ = 128


def local(tokens, w_gate_up, w_down, targets, proj_model, proj_hidden, store):
    n_z = lax.axis_size("z")
    n_core = lax.axis_size("core")
    n_t = lax.axis_size("tensor")
    z = lax.axis_index("z")
    core = lax.axis_index("core")
    t_idx = lax.axis_index("tensor")
    total = tokens.shape[0]
    rows_z = total // n_z
    rows_t = total // n_t
    width_ff = w_down.shape[0]
    width_h = width_ff // n_core
    hi = lax.Precision.HIGHEST
    tests = total // SEQ

    def over_dp(part):
        part = lax.psum_scatter(part.reshape(total, n_core, width_h), "core", scatter_dimension=1, tiled=False)
        part = lax.psum_scatter(part.astype(jnp.bfloat16), "z", scatter_dimension=0, tiled=True)
        return part.astype(jnp.float32)

    a_in_part = jnp.dot(tokens, proj_model[:, :RANK], preferred_element_type=jnp.float32)
    gate = over_dp(jnp.dot(tokens, w_gate_up[:, 0, :], preferred_element_type=jnp.float32))
    up = over_dp(jnp.dot(tokens, w_gate_up[:, 1, :], preferred_element_type=jnp.float32))
    sig = jax.nn.sigmoid(gate)
    act = gate * sig
    hidden_loc = (act * up).astype(jnp.bfloat16)
    hidden = lax.all_gather(hidden_loc, "z", axis=0, tiled=True)
    hidden = lax.all_gather(hidden, "core", axis=1, tiled=True)
    out_part = jnp.dot(hidden, w_down, preferred_element_type=jnp.float32)
    out_rows = lax.psum_scatter(out_part, "tensor", scatter_dimension=0, tiled=True)
    tgt_rows = lax.dynamic_slice_in_dim(targets, t_idx * rows_t, rows_t, 0)
    cot_rows = (out_rows - tgt_rows.astype(jnp.float32)).astype(jnp.bfloat16)
    cot = lax.all_gather(cot_rows, "tensor", axis=0, tiled=True)

    a_out_part = jnp.dot(cot, proj_model[:, RANK:], preferred_element_type=jnp.float32)
    side = lax.psum(jnp.concatenate([a_in_part, a_out_part], axis=1), ("z", "core"))

    dh = over_dp(lax.dot_general(cot, w_down, (((1,), (1,)), ((), ())), preferred_element_type=jnp.float32))
    dgate = (dh * up * sig * (1.0 + gate * (1.0 - sig))).astype(jnp.bfloat16)
    dup = (dh * act).astype(jnp.bfloat16)
    ph = lax.dynamic_slice_in_dim(proj_hidden, core * width_h, width_h, 0)
    b_part = jnp.concatenate(
        [
            jnp.dot(dgate, ph[:, :RANK], preferred_element_type=jnp.float32),
            jnp.dot(dup, ph[:, RANK : 2 * RANK], preferred_element_type=jnp.float32),
            jnp.dot(hidden_loc, ph[:, 2 * RANK :], preferred_element_type=jnp.float32),
        ],
        axis=1,
    )
    b_sum = lax.psum(b_part, ("core", "tensor"))
    side_z = lax.dynamic_slice_in_dim(side, z * rows_z, rows_z, 0)
    a_in = side_z[:, :RANK]
    a_out = side_z[:, RANK:]
    position = z * rows_z + lax.iota(jnp.int32, rows_z)
    member = ((position // SEQ)[:, None] == lax.iota(jnp.int32, tests)[None, :]).astype(jnp.float32)
    g_gate = jnp.einsum("ts,ti,tj->sij", member, a_in, b_sum[:, :RANK], precision=hi)
    g_up = jnp.einsum("ts,ti,tj->sij", member, a_in, b_sum[:, RANK : 2 * RANK], precision=hi)
    g_down = jnp.einsum("ts,ti,tj->sij", member, b_sum[:, 2 * RANK :], a_out, precision=hi)
    grads = lax.psum(jnp.stack([g_gate, g_up, g_down], axis=1).reshape(tests, 3 * RANK * RANK), "z")
    return lax.dot_general(
        grads.astype(jnp.bfloat16),
        store,
        (((1,), (1,)), ((), ())),
        preferred_element_type=jnp.float32,
    )


def solution(mesh):
    n_dp = mesh.shape["dp"]
    n_t = mesh.shape["tensor"]
    devices = np.asarray(mesh.devices).reshape(n_dp // 2, 2, n_t)
    fine = Mesh(devices, ("z", "core", "tensor"))
    dp = ("z", "core")
    return jax.shard_map(
        local,
        mesh=fine,
        in_specs=(
            P(None, dp),
            P(dp, None, "tensor"),
            P("tensor", dp),
            P(None, dp),
            P(dp, None),
            P("tensor", None),
            P(dp + ("tensor",), None),
        ),
        out_specs=P(None, dp + ("tensor",)),
        check_vma=False,
    )
```

time: 684 us -> 836 us (1.22)
  local copies, waits for them, and re-layouts: 33.4 us -> 195 us
  blocking collectives: 44.7 us -> 23.6 us
  other arithmetic: 3.62 us -> 22.2 us
  waiting for transfers between devices: 521 us -> 505 us
    dot_general x0 -> x2, local copies, waits for them, and re-layouts: none -> 121 us  [the longest x1 61.2 us: local(): jnp.dot(tokens, w_gate_up[:, 0, :], preferred_element_type=jnp.float32)]
    reduce_scatter x3 -> x7, waiting for transfers between devices: 383 us -> 282 us  [the longest x3 200 us: over_dp(): lax.psum_scatter(part.astype(jnp.bfloat16), 'z', scatter_dimension=0, til...]
    slice x0 -> x3, local copies, waits for them, and re-layouts: none -> 57.4 us  [the longest x1 55.9 us: local(): w_gate_up[:, 0, :]]
    all_gather x1 -> x3, waiting for transfers between devices: 71.9 us -> 117 us  [the longest x1 72.6 us: local(): hidden = lax.all_gather(hidden_loc, 'z', axis=0, tiled=True)]
    psum x1 -> x2, waiting for transfers between devices: 65.8 us -> 105 us  [the longest x1 52.7 us: local(): b_sum = lax.psum(b_part, ('core', 'tensor'))]
    convert_element_type x1 -> x5, other arithmetic: 3.45 us -> 20.7 us  [the longest x3 15.9 us: over_dp(): part.astype(jnp.bfloat16)]
    psum x1 -> x0, blocking collectives: 16.2 us -> none  [local(): lax.psum(hid_part.astype(jnp.bfloat16), 'tensor').astype(jnp.float32)]
    reshape x1, local copies, waits for them, and re-layouts: 29.6 us -> 14.3 us  [over_dp(): part.reshape(total, n_core, width_h)]
  transfers between devices with their start and end apart: 5 -> 12, of which waited for: 5 -> 11; matrix products, arithmetic and copies ran while one was open for 3% -> 12% of each run, Pallas kernels for 0% -> 0%
where the time goes in v2:
time: 836 us; the launch traced here: 831 us
  waiting for transfers between devices  505 us (60%)
  local copies, waits for them, and re-layouts  195 us (23%)
  matrix products  71.6 us (9%)
  blocking collectives  23.6 us (3%)
  other arithmetic  22.2 us (3%)
  between operations  13.7 us (2%)
    reduce_scatter x3, waiting for transfers between devices, over_dp(): lax.psum_scatter(part.astype(jnp.bfloat16), 'z', scatter_dimension=0, til...  200 us
    all_gather x1, waiting for transfers between devices, local(): hidden = lax.all_gather(hidden_loc, 'z', axis=0, tiled=True)  72.6 us
    dot_general x1, local copies, waits for them, and re-layouts, local(): jnp.dot(tokens, w_gate_up[:, 0, :], preferred_element_type=jnp.float32)  61.2 us
    dot_general x1, local copies, waits for them, and re-layouts, local(): jnp.dot(tokens, w_gate_up[:, 1, :], preferred_element_type=jnp.float32)  60 us
    slice x1, local copies, waits for them, and re-layouts, local(): w_gate_up[:, 0, :]  55.9 us
    psum x1, waiting for transfers between devices, local(): b_sum = lax.psum(b_part, ('core', 'tensor'))  52.7 us
    psum x1, waiting for transfers between devices, local(): lax.psum(jnp.concatenate([a_in_part, a_out_part], axis=1), ('z', 'core'))  52.3 us
    reduce_scatter x3, waiting for transfers between devices, over_dp(): lax.psum_scatter(part.reshape(total, n_core, width_h), 'core', scatter_di...  45.5 us
  transfers between devices with their start and end apart: 12, of which 11 were waited for; matrix products, arithmetic and copies ran while one was open for 12% of the time, Pallas kernels for 0%

profile of v2, /device:TPU:0, one launch (start us, length us, event | category | flops | bytes accessed | tf_op | source)
XLA Modules:
  0.0 831.2 jit_solution(7446013001953596638)
XLA Ops:
  6.5 55.9 %fusion.40 = (bf16[1024,1,7168]{2,1,0:T(2,128)(2,1)}, bf16[1024,1,7168]{2,1,0:T(2,128)(2,1)}) fusion(bf16[1024,2,7168]{2,1,0:T(2,128)(2,1)} %param.8), kind=kLoop, calls=%fused_computation.63 | loop fusion | bytes 58720256 | tf_op jit(solution)/shard_map/slice | solution.py:32
  62.4 60.0 %copy.21 = bf16[1024,1,7168]{0,2,1:T(8,128)(2,1)} copy(bf16[1024,1,7168]{2,1,0:T(2,128)(2,1)} %get-tuple-element.6) | data formatting | bytes 29360128 | tf_op jit(solution)/shard_map/dot_general | solution.py:33
  122.4 14.3 %fusion.9 = f32[512,2,3584]{2,0,1:T(8,128)} fusion(bf16[2,3584,1024]{2,1,0:T(8,128)(2,1)} %bitcast.58, bf16[512,1024]{1,0:T(8,128)(2,1)} %param.7), kind=kOutput, calls=%fused_computation.21 | convolution fusion | flops 7516192768 | bytes 30408704 | tf_op jit(solution)/shard_map/dot_general | solution.py:33
  136.7 0.0 reduce-scatter.12.cloned.1.call-update
  136.7 0.0 reduce-scatter.8.cloned.1.call-start
  136.8 61.2 %copy.20 = bf16[1024,1,7168]{0,2,1:T(8,128)(2,1)} copy(bf16[1024,1,7168]{2,1,0:T(2,128)(2,1)} %get-tuple-element.5) | data formatting | bytes 29360128 | tf_op jit(solution)/shard_map/dot_general | solution.py:32
  198.0 14.4 %fusion.11 = f32[512,2,3584]{2,0,1:T(8,128)} fusion(bf16[2,3584,1024]{2,1,0:T(8,128)(2,1)} %bitcast.59, bf16[512,1024]{1,0:T(8,128)(2,1)} %param.7), kind=kOutput, calls=%fused_computation.23 | convolution fusion | flops 7516192768 | bytes 30408704 | tf_op jit(solution)/shard_map/dot_general | solution.py:32
  212.3 0.0 reduce-scatter.8.cloned.1.call-update
  212.4 0.0 reduce-scatter.14.cloned.1.call-start
  212.4 0.0 reduce-scatter.12.cloned.1.call-done
  212.4 5.4 convert_bitcast_fusion.1
  217.8 0.0 reduce-scatter.14.cloned.1.call-update
  217.8 0.0 reduce-scatter.10.cloned.1.call-start
  217.9 21.3 %reduce-scatter.8.cloned.1.call-done = f32[512,1,3584]{2,0,1:T(8,128)} async-done(((f32[512,2,3584]{2,0,1:T(8,128)}), f32[512,1,3584]{2,0,1:T(8,128)}) %reduce-scatter.8.cloned.1.call-update) | async-done | bytes 7340048 | tf_op jit(solution)/shard_map/reduce_scatter | solution.py:27
  239.2 5.3 convert_bitcast_fusion.2
  244.5 0.0 reduce-scatter.10.cloned.1.call-update
  244.5 0.0 all-gather.4.cloned.1.call-start
  244.6 66.6 %reduce-scatter.14.cloned.1.call-done = bf16[128,3584]{1,0:T(8,128)(2,1)} async-done(((bf16[512,3584]{1,0:T(8,128)(2,1)}), bf16[128,3584]{1,0:T(8,128)(2,1)}) %reduce-scatter.14.cloned.1.call-update) | async-done | bytes 917520 | tf_op jit(solution)/shard_map/reduce_scatter | solution.py:28
  311.1 71.0 %reduce-scatter.10.cloned.1.call-done = bf16[128,3584]{1,0:T(8,128)(2,1)} async-done(((bf16[512,3584]{1,0:T(8,128)(2,1)}), bf16[128,3584]{1,0:T(8,128)(2,1)}) %reduce-scatter.10.cloned.1.call-update) | async-done | bytes 917520 | tf_op jit(solution)/shard_map/reduce_scatter | solution.py:28
  382.1 2.9 fusion
  385.0 0.0 all-gather.4.cloned.1.call-update
  385.0 0.0 all-gather.6.cloned.1.call-start
  385.1 72.6 %all-gather.4.cloned.1.call-done = bf16[512,3584]{1,0:T(8,128)(2,1)} async-done(((bf16[128,3584]{1,0:T(8,128)(2,1)}), bf16[512,3584]{1,0:T(8,128)(2,1)}) %all-gather.4.cloned.1.call-update) | async-done | bytes 3670032 | tf_op jit(solution)/shard_map/all_gather | solution.py:37
  457.7 0.0 all-gather.6.cloned.1.call-update
  457.7 0.2 reduce-scatter.16.cloned.1.call-start
  458.0 18.1 %all-gather.6.cloned.1.call-done = bf16[512,7168]{1,0:T(8,128)(2,1)} async-done(((bf16[512,3584]{1,0:T(8,128)(2,1)}), bf16[512,7168]{1,0:T(8,128)(2,1)}) %all-gather.6.cloned.1.call-update) | async-done | bytes 7340048 | tf_op jit(solution)/shard_map/all_gather | solution.py:38
  476.1 14.1 %fusion.41 = f32[512,1024]{1,0:T(8,128)} fusion(bf16[512,7168]{1,0:T(8,128)(2,1)} %all-gather.6.cloned.1.call-done, bf16[7168,1024]{1,0:T(8,128)(2,1)} %param.9), kind=kOutput, calls=%fused_computation.64 | convolution fusion | flops 7516192768 | bytes 24117248 | tf_op jit(solution)/shard_map/dot_general | solution.py:39
  490.2 0.0 reduce-scatter.16.cloned.1.call-update
  490.2 0.0 all-gather.8.cloned.1.call-start
  490.3 36.5 %reduce-scatter.16.cloned.1.call-done = f32[128,1024]{1,0:T(8,128)} async-done(((f32[512,1024]{1,0:T(8,128)}), f32[128,1024]{1,0:T(8,128)}) %reduce-scatter.16.cloned.1.call-update) | async-done | bytes 524304 | tf_op jit(solution)/shard_map/reduce_scatter | solution.py:40
  526.7 1.9 subtract_convert_fusion
  528.6 0.0 all-gather.8.cloned.1.call-update
  528.6 0.0 reduce-scatter.18.cloned.1.call-start
  528.7 26.7 %all-gather.8.cloned.1.call-done = bf16[512,1024]{1,0:T(8,128)(2,1)} async-done(((bf16[128,1024]{1,0:T(8,128)(2,1)}), bf16[512,1024]{1,0:T(8,128)(2,1)}) %all-gather.8.cloned.1.call-update) | async-done | bytes 1048592 | tf_op jit(solution)/shard_map/all_gather | solution.py:43
  555.4 14.4 %fusion.42 = f32[512,7168]{0,1:T(8,128)} fusion(bf16[512,1024]{1,0:T(8,128)(2,1)} %all-gather.8.cloned.1.call-done, bf16[7168,1024]{1,0:T(8,128)(2,1)} %param.9), kind=kOutput, calls=%fused_computation.65 | convolution fusion | flops 7516192768 | bytes 30408704 | tf_op jit(solution)/shard_map/dot_general | solution.py:48
  569.8 14.3 %copy.15 = f32[512,2,3584]{2,0,1:T(8,128)} copy(f32[512,2,3584]{0,2,1:T(8,128)} %bitcast.60) | data formatting | bytes 29360128 | tf_op jit(solution)/shard_map/reshape | solution.py:27
  584.1 0.0 reduce-scatter.18.cloned.1.call-update
  584.1 0.0 reduce-scatter.20.cloned.1.call-start
  584.2 24.1 %reduce-scatter.18.cloned.1.call-done = f32[512,1,3584]{2,0,1:T(8,128)} async-done(((f32[512,2,3584]{2,0,1:T(8,128)}), f32[512,1,3584]{2,0,1:T(8,128)}) %reduce-scatter.18.cloned.1.call-update) | async-done | bytes 7340048 | tf_op jit(solution)/shard_map/reduce_scatter | solution.py:27
  608.3 5.3 convert_bitcast_fusion
  613.6 0.0 reduce-scatter.20.cloned.1.call-update
  613.6 0.0 all-reduce.4.cloned.1.call-start
  613.7 0.8 copy-done.1
  614.5 1.7 fusion.23
  616.2 1.7 fusion.17
  617.9 1.7 fusion.21
  619.6 0.7 pad_maximum_fusion.1
  620.4 0.0 all-reduce.4.cloned.1.call-update
  620.4 0.0 all-reduce.6.cloned.1.call-start
  620.4 62.9 %reduce-scatter.20.cloned.1.call-done = bf16[128,3584]{1,0:T(8,128)(2,1)} async-done(((bf16[512,3584]{1,0:T(8,128)(2,1)}), bf16[128,3584]{1,0:T(8,128)(2,1)}) %reduce-scatter.20.cloned.1.call-update) | async-done | bytes 917520 | tf_op jit(solution)/shard_map/reduce_scatter | solution.py:28
  683.3 3.0 fusion.15
  686.3 1.8 fusion.13
  688.1 0.7 pad_maximum_fusion.2
  688.7 0.0 all-reduce.6.cloned.1.call-update
  688.7 52.3 %all-reduce.4.cloned.1.call-done = f32[512,128]{0,1:T(8,128)} async-done(((f32[512,128]{0,1:T(8,128)}), f32[512,128]{0,1:T(8,128)}) %all-reduce.4.cloned.1.call-update) | async-done | bytes 262160 | tf_op jit(solution)/shard_map/psum | solution.py:46
  741.1 0.8 constant_dynamic-slice_fusion
  741.8 52.7 %all-reduce.6.cloned.1.call-done = f32[128,192]{0,1:T(8,128)} async-done(((f32[128,192]{0,1:T(8,128)}), f32[128,192]{0,1:T(8,128)}) %all-reduce.6.cloned.1.call-update) | async-done | bytes 98320 | tf_op jit(solution)/shard_map/psum | solution.py:60
  794.5 0.8 slice.50
  795.2 1.0 convolution_bitcast_fusion.1
  796.3 1.0 convolution_bitcast_fusion.2
  797.3 1.0 convolution_bitcast_fusion
  798.4 0.9 reshape.33
  799.2 23.6 %all-reduce.7 = bf16[4,12288]{1,0:T(4,128)(2,1)S(1)} all-reduce(f32[4,12288]{1,0:T(4,128)} %reshape.33), channel_id=1, replica_groups=mesh['z'=4,'core'=2,'tensor'=4] {'z'}, use_global_device_ids=true, to_apply=%region_9.10 | all-reduce | flops 49152 | bytes 294912 | tf_op jit(solution)/shard_map/psum | solution.py:69
  822.9 1.5 fusion.43
  (12 shorter events, 0.1 us)
Async XLA Ops:
  6.5 816.3 %copy-start = (bf16[128,12288]{1,0:T(8,128)(2,1)S(1)}, bf16[128,12288]{1,0:T(8,128)(2,1)}, u32[]{:S(2)}) copy-start(bf16[128,12288]{1,0:T(8,128)(2,1)} %param.13) | copy-start | bytes 9437188
  6.5 205.9 %reduce-scatter.12.cloned.1.call-start = ((), (), s32[]{:S(2)}) async-start(), calls=%async_computation.9 | async-start | bytes 22020096 | tf_op jit(solution)/shard_map/reduce_scatter | solution.py:27
  136.7 102.5 %reduce-scatter.8.cloned.1.call-start = ((), (), s32[]{:S(2)}) async-start(), calls=%async_computation.7 | async-start | bytes 22020096 | tf_op jit(solution)/shard_map/reduce_scatter | solution.py:27
  212.4 98.7 %reduce-scatter.14.cloned.1.call-start = ((), (), s32[]{:S(2)}) async-start(), calls=%async_computation.10 | async-start | bytes 4587520 | tf_op jit(solution)/shard_map/reduce_scatter | solution.py:28
  217.8 164.2 %reduce-scatter.10.cloned.1.call-start = ((), (), s32[]{:S(2)}) async-start(), calls=%async_computation.8 | async-start | bytes 4587520 | tf_op jit(solution)/shard_map/reduce_scatter | solution.py:28
  244.5 213.2 %all-gather.4.cloned.1.call-start = ((), (), s32[]{:S(2)}) async-start(), calls=%async_computation.11 | async-start | bytes 4587520 | tf_op jit(solution)/shard_map/all_gather | solution.py:37
  385.0 91.0 %all-gather.6.cloned.1.call-start = ((), (), s32[]{:S(2)}) async-start(), calls=%async_computation.12 | async-start | bytes 11010048 | tf_op jit(solution)/shard_map/all_gather | solution.py:38
  457.7 69.0 %reduce-scatter.16.cloned.1.call-start = ((), (), s32[]{:S(2)}) async-start(), calls=%async_computation.13 | async-start | bytes 2621440 | tf_op jit(solution)/shard_map/reduce_scatter | solution.py:40
  490.2 65.2 %all-gather.8.cloned.1.call-start = ((), (), s32[]{:S(2)}) async-start(), calls=%async_computation.14 | async-start | bytes 1310720 | tf_op jit(solution)/shard_map/all_gather | solution.py:43
  528.6 79.6 %reduce-scatter.18.cloned.1.call-start = ((), (), s32[]{:S(2)}) async-start(), calls=%async_computation.16 | async-start | bytes 22020096 | tf_op jit(solution)/shard_map/reduce_scatter | solution.py:27
  584.1 99.2 %reduce-scatter.20.cloned.1.call-start = ((), (), s32[]{:S(2)}) async-start(), calls=%async_computation.17 | async-start | bytes 4587520 | tf_op jit(solution)/shard_map/reduce_scatter | solution.py:28
  613.6 0.9 copy-start.1
  613.6 127.5 %all-reduce.4.cloned.1.call-start = ((), (), s32[]{:S(2)}) async-start(), calls=%async_computation.15 | async-start | bytes 524288 | tf_op jit(solution)/shard_map/psum | solution.py:46
  620.4 174.1 %all-reduce.6.cloned.1.call-start = ((), (), s32[]{:S(2)}) async-start(), calls=%async_computation.18 | async-start | bytes 196608 | tf_op jit(solution)/shard_map/psum | solution.py:60
  683.3 3.0 copy-start.2
  683.3 3.0 copy-start.3
Sparse Core Ops, SparseCore 0:
  136.8 26.6 reduce-scatter.11
  212.5 26.6 reduce-scatter.7
  241.5 69.5 reduce-scatter.13
  313.3 68.7 reduce-scatter.9
  385.2 72.4 all-gather.3
  459.1 16.9 all-gather.5
  490.3 36.3 reduce-scatter.15
  528.7 26.6 all-gather.7
  584.2 23.9 reduce-scatter.17
  613.7 69.5 reduce-scatter.19
  685.7 55.2 all-reduce.3
  744.0 50.4 all-reduce.5

commit v3 on v0

v3 whole, which is shorter than its diff:
```python
import jax
import jax.numpy as jnp
from jax import lax
from jax.sharding import PartitionSpec as P

RANK = 64
SEQ = 128


def local(tokens, w_gate_up, w_down, targets, proj_model, proj_hidden, store):
    total = tokens.shape[0]
    hi = lax.Precision.HIGHEST
    tests = total // SEQ
    a_in_part = jnp.dot(tokens, proj_model[:, :RANK], preferred_element_type=jnp.float32)
    n_dp = lax.axis_size("dp")
    rows = total // n_dp
    width_ff = w_down.shape[0]
    both = jnp.einsum("td,dkf->ktf", tokens, w_gate_up, preferred_element_type=jnp.float32)
    both = both.astype(jnp.bfloat16).reshape(2, n_dp, rows, width_ff).transpose(1, 0, 2, 3)
    gate_up = lax.psum_scatter(
        both.reshape(n_dp * 2 * rows, width_ff), "dp", scatter_dimension=0, tiled=True
    ).astype(jnp.float32).reshape(2, rows, width_ff)
    gate = gate_up[0]
    up = gate_up[1]
    sig = jax.nn.sigmoid(gate)
    act = gate * sig
    hidden = (act * up).astype(jnp.bfloat16)
    out_part = jnp.dot(
        lax.all_gather(hidden, "dp", axis=0, tiled=True), w_down, preferred_element_type=jnp.float32
    )
    out_full = lax.psum(out_part, "tensor")
    cot = (out_full - targets.astype(jnp.float32)).astype(jnp.bfloat16)
    a_out_part = jnp.dot(cot, proj_model[:, RANK:], preferred_element_type=jnp.float32)
    side = lax.psum(jnp.concatenate([a_in_part, a_out_part], axis=1), "dp")
    grad_hidden = lax.psum_scatter(
        lax.dot_general(
            cot, w_down, (((1,), (1,)), ((), ())), preferred_element_type=jnp.float32
        ),
        "dp",
        scatter_dimension=0,
        tiled=True,
    )
    dgate = (grad_hidden * up * sig * (1.0 + gate * (1.0 - sig))).astype(jnp.bfloat16)
    dup = (grad_hidden * act).astype(jnp.bfloat16)
    hid_part = jnp.concatenate(
        [
            jnp.dot(dgate, proj_hidden[:, :RANK], preferred_element_type=jnp.float32),
            jnp.dot(dup, proj_hidden[:, RANK : 2 * RANK], preferred_element_type=jnp.float32),
            jnp.dot(hidden, proj_hidden[:, 2 * RANK :], preferred_element_type=jnp.float32),
        ],
        axis=1,
    )
    hid_sum = lax.all_gather(lax.psum(hid_part, "tensor"), "dp", axis=0, tiled=True)
    a_in = side[:, :RANK]
    a_out = side[:, RANK:]
    position = lax.iota(jnp.int32, total)
    member = ((position // SEQ)[:, None] == lax.iota(jnp.int32, tests)[None, :]).astype(jnp.float32)
    g_gate = jnp.einsum("ts,ti,tj->sij", member, a_in, hid_sum[:, :RANK], precision=hi)
    g_up = jnp.einsum("ts,ti,tj->sij", member, a_in, hid_sum[:, RANK : 2 * RANK], precision=hi)
    g_down = jnp.einsum("ts,ti,tj->sij", member, hid_sum[:, 2 * RANK :], a_out, precision=hi)
    grads = jnp.stack([g_gate, g_up, g_down], axis=1).reshape(tests, 3 * RANK * RANK)
    return lax.dot_general(
        grads.astype(jnp.bfloat16),
        store,
        (((1,), (1,)), ((), ())),
        preferred_element_type=jnp.float32,
    )


def solution(mesh):
    return jax.shard_map(
        local,
        mesh=mesh,
        in_specs=(
            P(None, "dp"),
            P("dp", None, "tensor"),
            P("tensor", "dp"),
            P(None, "dp"),
            P("dp", None),
            P("tensor", None),
            P(("dp", "tensor"), None),
        ),
        out_specs=P(None, ("dp", "tensor")),
        check_vma=False,
    )
```

time: 684 us -> 617 us (0.902)
  waiting for transfers between devices: 521 us -> 477 us
  local copies, waits for them, and re-layouts: 33.4 us -> 18.2 us
  blocking collectives: 44.7 us -> 31.7 us
    reduce_scatter x3 -> x2, waiting for transfers between devices: 383 us -> 301 us  [the longest x1 152 us: local(): lax.psum_scatter(both.reshape(n_dp * 2 * rows, width_ff), 'dp', scatter_d...]
    psum x0 -> x1, waiting for transfers between devices: none -> 38.1 us  [local(): side = lax.psum(jnp.concatenate([a_in_part, a_out_part], axis=1), 'dp')]
    reshape x2 -> x0, local copies, waits for them, and re-layouts: 30.4 us -> none  [the longest x1 29.6 us: local(): both.reshape(tok_rows * lax.axis_size('dp'), 2 * width_ff)]
    psum x2 -> x1, blocking collectives: 44.7 us -> 16.9 us  [local(): lax.psum(hid_part, 'tensor')]
    all_gather x0 -> x1, blocking collectives: none -> 14.8 us  [local(): lax.all_gather(lax.psum(hid_part, 'tensor'), 'dp', axis=0, tiled=True)]
    transpose x0 -> x1, local copies, waits for them, and re-layouts: none -> 13.5 us  [local(): both.astype(jnp.bfloat16).reshape(2, n_dp, rows, width_ff)]
where the time goes in v3:
time: 617 us; the launch traced here: 616 us
  waiting for transfers between devices  477 us (77%)
  matrix products  71 us (12%)
  blocking collectives  31.7 us (5%)
  local copies, waits for them, and re-layouts  18.2 us (3%)
  between operations  13.2 us (2%)
    reduce_scatter x1, waiting for transfers between devices, local(): lax.psum_scatter(both.reshape(n_dp * 2 * rows, width_ff), 'dp', scatter_d...  152 us
    reduce_scatter x1, waiting for transfers between devices, local(): lax.psum_scatter(lax.dot_general(cot, w_down, (((1,), (1,)), ((), ())), p...  149 us
    all_gather x1, waiting for transfers between devices, local(): lax.all_gather(hidden, 'dp', axis=0, tiled=True)  71.8 us
    psum x1, waiting for transfers between devices, local(): out_full = lax.psum(out_part, 'tensor')  65.8 us
    psum x1, waiting for transfers between devices, local(): side = lax.psum(jnp.concatenate([a_in_part, a_out_part], axis=1), 'dp')  38.1 us
    dot_general x1, matrix products, local(): jnp.einsum('td,dkf->ktf', tokens, w_gate_up, preferred_element_type=jnp.f...  24.9 us
    psum x1, blocking collectives, local(): lax.psum(hid_part, 'tensor')  16.9 us
    dot_general x1, matrix products, local(): lax.dot_general(cot, w_down, (((1,), (1,)), ((), ())), preferred_element_...  14.9 us
  transfers between devices with their start and end apart: 5, of which 5 were waited for; matrix products, arithmetic and copies ran while one was open for 3% of the time, Pallas kernels for 0%

profile of v3, /device:TPU:0, one launch (start us, length us, event | category | flops | bytes accessed | tf_op | source)
XLA Modules:
  0.0 616.4 jit_solution(7169694522479102521)
XLA Ops:
  6.5 0.0 copy-start
  6.5 0.0 reduce-scatter.3.cloned.1.call-start
  6.5 24.9 %fusion.2 = bf16[2,7168,512]{1,2,0:T(8,128)(2,1)} fusion(bf16[1024,2,7168]{2,1,0:T(2,128)(2,1)} %param.8, bf16[512,1024]{1,0:T(8,128)(2,1)} %param.7), kind=kOutput, calls=%fused_computation.2 | convolution fusion | flops 15039725568 | bytes 45088768 | tf_op jit(solution)/shard_map/td,dkf->ktf/dot_general | solution.py:18
  31.4 13.5 %copy.14 = bf16[8,2,64,7168]{3,2,1,0:T(8,128)(2,1)} copy(bf16[8,2,64,7168]{3,2,0,1:T(8,128)(2,1)} %bitcast.40) | data formatting | bytes 29360128 | tf_op jit(solution)/shard_map/transpose | solution.py:19
  44.9 0.0 reduce-scatter.3.cloned.1.call-update
  45.0 0.0 all-gather.2.cloned.1.call-start
  45.0 151.8 %reduce-scatter.3.cloned.1.call-done = bf16[128,7168]{1,0:T(8,128)(2,1)} async-done(((bf16[1024,7168]{1,0:T(8,128)(2,1)}), bf16[128,7168]{1,0:T(8,128)(2,1)}) %reduce-scatter.3.cloned.1.call-update) | async-done | bytes 1835024 | tf_op jit(solution)/shard_map/reduce_scatter | solution.py:20
  196.8 1.9 convert_element_type.31
  198.7 0.0 copy-start.1
  198.7 1.8 copy-done.1
  200.5 1.4 multiply_convert_fusion.2
  201.9 0.0 all-gather.2.cloned.1.call-update
  201.9 0.0 all-reduce.3.cloned.1.call-start
  202.0 71.8 %all-gather.2.cloned.1.call-done = bf16[512,7168]{1,0:T(8,128)(2,1)} async-done(((bf16[64,7168]{1,0:T(8,128)(2,1)}), bf16[512,7168]{1,0:T(8,128)(2,1)}) %all-gather.2.cloned.1.call-update) | async-done | bytes 7340048 | tf_op jit(solution)/shard_map/all_gather | solution.py:29
  273.8 14.3 %fusion.37 = f32[512,1024]{1,0:T(8,128)} fusion(bf16[512,7168]{1,0:T(8,128)(2,1)} %all-gather.2.cloned.1.call-done, bf16[7168,1024]{1,0:T(8,128)(2,1)} %param.9), kind=kOutput, calls=%fused_computation.53 | convolution fusion | flops 7516192768 | bytes 24117248 | tf_op jit(solution)/shard_map/dot_general | solution.py:28
  288.1 0.0 copy-start.3
  288.1 0.0 all-reduce.3.cloned.1.call-update
  288.1 0.0 all-reduce.5.cloned.1.call-start
  288.2 0.9 copy-done.3
  289.1 1.7 fusion.27
  290.7 65.8 %all-reduce.3.cloned.1.call-done = f32[512,1024]{1,0:T(8,128)} async-done(((f32[512,1024]{1,0:T(8,128)}), f32[512,1024]{1,0:T(8,128)}) %all-reduce.3.cloned.1.call-update) | async-done | bytes 2097168 | tf_op jit(solution)/shard_map/psum | solution.py:31
  356.5 2.4 fusion.25
  358.9 0.7 pad_maximum_fusion
  359.6 0.0 all-reduce.5.cloned.1.call-update
  359.7 0.2 reduce-scatter.5.cloned.1.call-start
  359.9 14.9 %fusion.36 = f32[512,7168]{1,0:T(8,128)} fusion(bf16[7168,1024]{1,0:T(8,128)(2,1)} %param.9, f32[512,1024]{1,0:T(8,128)} %all-reduce.3.cloned.1.call-done, bf16[512,1024]{1,0:T(8,128)(2,1)} %param.10), kind=kOutput, calls=%fused_computation.52 | convolution fusion | flops 7517765632 | bytes 32505856 | tf_op jit(solution)/shard_map/dot_general | solution.py:36
  374.8 0.0 reduce-scatter.5.cloned.1.call-update
  374.8 1.8 fusion.11
  376.7 38.1 %all-reduce.5.cloned.1.call-done = f32[512,128]{0,1:T(8,128)} async-done(((f32[512,128]{0,1:T(8,128)}), f32[512,128]{0,1:T(8,128)}) %all-reduce.5.cloned.1.call-update) | async-done | bytes 262160 | tf_op jit(solution)/shard_map/psum | solution.py:34
  414.8 0.9 slice.52
  415.7 149.3 %reduce-scatter.5.cloned.1.call-done = f32[64,7168]{1,0:T(8,128)} async-done(((f32[512,7168]{1,0:T(8,128)}), f32[64,7168]{1,0:T(8,128)}) %reduce-scatter.5.cloned.1.call-update) | async-done | bytes 1835024 | tf_op jit(solution)/shard_map/reduce_scatter | solution.py:35
  565.0 0.0 copy-start.2
  565.0 0.0 copy-start.4
  565.0 3.8 fusion.14
  568.8 0.1 copy-done.2
  569.0 0.6 copy-done.4
  569.5 1.8 fusion.10
  571.4 0.1 pad_maximum_fusion.2
  571.5 16.9 %psum.23 = f32[64,192]{1,0:T(8,128)S(1)} all-reduce(f32[64,192]{1,0:T(8,128)S(1)} %pad_maximum_fusion.2), channel_id=1, replica_groups=mesh['dp'=8,'tensor'=4] {'tensor'}, use_global_device_ids=true, to_apply=%region_4.0 | all-reduce | flops 12288 | bytes 98304 | tf_op jit(solution)/shard_map/psum | solution.py:53
  588.3 14.8 %all_gather.7 = f32[512,192]{1,0:T(8,128)S(1)} all-gather(f32[64,192]{1,0:T(8,128)S(1)} %psum.23), channel_id=1, replica_groups=mesh['dp'=8,'tensor'=4] {'dp'}, dimensions={0}, use_global_device_ids=true | all-gather | bytes 442368 | tf_op jit(solution)/shard_map/all_gather | solution.py:53
  603.2 1.2 fusion.6
  604.4 1.3 fusion.7
  605.7 0.1 copy.17
  605.8 1.5 fusion.8
  607.3 0.9 pad_maximum_fusion.1
  608.2 0.2 convert_element_type.37
  608.4 0.0 copy-done
  608.4 1.5 fusion.38
  (4 shorter events, 0.0 us)
Async XLA Ops:
  6.5 601.9 %copy-start = (bf16[128,12288]{1,0:T(8,128)(2,1)S(1)}, bf16[128,12288]{1,0:T(8,128)(2,1)}, u32[]{:S(2)}) copy-start(bf16[128,12288]{1,0:T(8,128)(2,1)} %param.13) | copy-start | bytes 9437188
  6.5 190.3 %reduce-scatter.3.cloned.1.call-start = ((), (), s32[]{:S(2)}) async-start(), calls=%async_computation.2 | async-start | bytes 16515072 | tf_op jit(solution)/shard_map/reduce_scatter | solution.py:20
  45.0 228.8 %all-gather.2.cloned.1.call-start = ((), (), s32[]{:S(2)}) async-start(), calls=%async_computation.3 | async-start | bytes 8257536 | tf_op jit(solution)/shard_map/all_gather | solution.py:29
  198.7 1.8 copy-start.1
  201.9 154.6 %all-reduce.3.cloned.1.call-start = ((), (), s32[]{:S(2)}) async-start(), calls=%async_computation.4 | async-start | bytes 4194304 | tf_op jit(solution)/shard_map/psum | solution.py:31
  288.1 0.9 copy-start.3
  288.1 126.7 %all-reduce.5.cloned.1.call-start = ((), (), s32[]{:S(2)}) async-start(), calls=%async_computation.5 | async-start | bytes 524288 | tf_op jit(solution)/shard_map/psum | solution.py:34
  359.7 205.3 %reduce-scatter.5.cloned.1.call-start = ((), (), s32[]{:S(2)}) async-start(), calls=%async_computation.6 | async-start | bytes 16515072 | tf_op jit(solution)/shard_map/reduce_scatter | solution.py:35
  565.0 3.9 copy-start.2
  565.0 4.5 copy-start.4
Sparse Core Ops, SparseCore 0:
  45.1 151.6 reduce-scatter.2
  202.0 71.7 all-gather.1
  288.3 68.2 all-reduce.2
  359.8 54.9 all-reduce.4
  417.0 147.9 reduce-scatter.4

commit v4 on v3

v4 whole, which is shorter than its diff:
```python
import jax
import jax.numpy as jnp
from jax import lax
import numpy as np
from jax.sharding import Mesh, PartitionSpec as P

RANK = 64
SEQ = 128
DP = ("z", "core")


def local(tokens, w_gate_up, w_down, targets, proj_model, proj_hidden, store):
    total = tokens.shape[0]
    hi = lax.Precision.HIGHEST
    tests = total // SEQ
    a_in_part = jnp.dot(tokens, proj_model[:, :RANK], preferred_element_type=jnp.float32)
    n_z = lax.axis_size("z")
    n_core = lax.axis_size("core")
    rows_z = total // n_z
    width_ff = w_down.shape[0]
    width_h = width_ff // n_core
    both = jnp.einsum("td,dkf->tkf", tokens, w_gate_up, preferred_element_type=jnp.float32)
    both = both.reshape(total, 2, n_core, width_h)
    both = lax.psum_scatter(both, "core", scatter_dimension=2, tiled=False)
    one = 1.0 + 0.0 * lax.axis_index("z").astype(jnp.float32)
    both = lax.psum_scatter(
        (both * one).astype(jnp.bfloat16), "z", scatter_dimension=0, tiled=True
    ).astype(jnp.float32)
    gate_up = lax.all_to_all(both, "core", 0, 2, tiled=True)
    gate = gate_up[:, 0]
    up = gate_up[:, 1]
    sig = jax.nn.sigmoid(gate)
    act = gate * sig
    hidden = (act * up).astype(jnp.bfloat16)
    out_part = jnp.dot(
        lax.all_gather(hidden, DP, axis=0, tiled=True), w_down, preferred_element_type=jnp.float32
    )
    out_full = lax.psum(out_part, "tensor")
    cot = (out_full - targets.astype(jnp.float32)).astype(jnp.bfloat16)
    a_out_part = jnp.dot(cot, proj_model[:, RANK:], preferred_element_type=jnp.float32)
    side = lax.psum(jnp.concatenate([a_in_part, a_out_part], axis=1), DP)
    grad_hidden = lax.psum_scatter(
        lax.dot_general(
            cot, w_down, (((1,), (1,)), ((), ())), preferred_element_type=jnp.float32
        ).astype(jnp.bfloat16),
        DP,
        scatter_dimension=0,
        tiled=True,
    ).astype(jnp.float32)
    dgate = (grad_hidden * up * sig * (1.0 + gate * (1.0 - sig))).astype(jnp.bfloat16)
    dup = (grad_hidden * act).astype(jnp.bfloat16)
    hid_part = jnp.concatenate(
        [
            jnp.dot(dgate, proj_hidden[:, :RANK], preferred_element_type=jnp.float32),
            jnp.dot(dup, proj_hidden[:, RANK : 2 * RANK], preferred_element_type=jnp.float32),
            jnp.dot(hidden, proj_hidden[:, 2 * RANK :], preferred_element_type=jnp.float32),
        ],
        axis=1,
    )
    hid_sum = lax.all_gather(lax.psum(hid_part, "tensor"), DP, axis=0, tiled=True)
    a_in = side[:, :RANK]
    a_out = side[:, RANK:]
    position = lax.iota(jnp.int32, total)
    member = ((position // SEQ)[:, None] == lax.iota(jnp.int32, tests)[None, :]).astype(jnp.float32)
    g_gate = jnp.einsum("ts,ti,tj->sij", member, a_in, hid_sum[:, :RANK], precision=hi)
    g_up = jnp.einsum("ts,ti,tj->sij", member, a_in, hid_sum[:, RANK : 2 * RANK], precision=hi)
    g_down = jnp.einsum("ts,ti,tj->sij", member, hid_sum[:, 2 * RANK :], a_out, precision=hi)
    grads = jnp.stack([g_gate, g_up, g_down], axis=1).reshape(tests, 3 * RANK * RANK)
    return lax.dot_general(
        grads.astype(jnp.bfloat16),
        store,
        (((1,), (1,)), ((), ())),
        preferred_element_type=jnp.float32,
    )


def solution(mesh):
    n_dp = mesh.shape["dp"]
    n_t = mesh.shape["tensor"]
    devices = np.asarray(mesh.devices).reshape(n_dp // 2, 2, n_t)
    fine = Mesh(devices, ("z", "core", "tensor"))
    return jax.shard_map(
        local,
        mesh=fine,
        in_specs=(
            P(None, DP),
            P(DP, None, "tensor"),
            P("tensor", DP),
            P(None, DP),
            P(DP, None),
            P("tensor", None),
            P(DP + ("tensor",), None),
        ),
        out_specs=P(None, DP + ("tensor",)),
        check_vma=False,
    )
```

time: 617 us -> 663 us (1.075)
  local copies, waits for them, and re-layouts: 18.2 us -> 39.2 us
  other arithmetic: 5.01 us -> 15.8 us
  blocking collectives: 31.7 us -> 38.4 us
    unnamed x5 -> x7, waiting for transfers between devices: 0.08 us -> 93.3 us
    reduce_scatter x1, waiting for transfers between devices: 149 us -> 80 us  [local(): lax.psum_scatter(lax.dot_general(cot, w_down, (((1,), (1,)), ((), ())), p...]
    reduce_scatter x1, waiting for transfers between devices: 152 us -> 129 us  [local(): lax.psum_scatter((both * one).astype(jnp.bfloat16), 'z', scatter_dimensio...]
    reshape x0 -> x1, local copies, waits for them, and re-layouts: none -> 22.3 us  [local(): both = both.reshape(total, 2, n_core, width_h)]
    transpose x1 -> x0, local copies, waits for them, and re-layouts: 13.5 us -> none  [local(): both.astype(jnp.bfloat16).reshape(2, n_dp, rows, width_ff)]
    all_to_all x0 -> x2, local copies, waits for them, and re-layouts: none -> 10.7 us  [local(): gate_up = lax.all_to_all(both, 'core', 0, 2, tiled=True)]
    convert_element_type x1, other arithmetic: 1.85 us -> 10.6 us  [local(): (both * one).astype(jnp.bfloat16)]
    all_to_all x0 -> x1, blocking collectives: none -> 6.68 us  [local(): gate_up = lax.all_to_all(both, 'core', 0, 2, tiled=True)]
  transfers between devices with their start and end apart: 5 -> 6, of which waited for: 5 -> 6; matrix products, arithmetic and copies ran while one was open for 3% -> 3% of each run, Pallas kernels for 0% -> 0%
where the time goes in v4:
time: 663 us; the launch traced here: 662 us
  waiting for transfers between devices  482 us (73%)
  matrix products  72.5 us (11%)
  local copies, waits for them, and re-layouts  39.2 us (6%)
  blocking collectives  38.4 us (6%)
  other arithmetic  15.8 us (2%)
  between operations  13.6 us (2%)
    reduce_scatter x1, waiting for transfers between devices, local(): lax.psum_scatter((both * one).astype(jnp.bfloat16), 'z', scatter_dimensio...  129 us
    unnamed x7, waiting for transfers between devices  93.3 us
    reduce_scatter x1, waiting for transfers between devices, local(): lax.psum_scatter(lax.dot_general(cot, w_down, (((1,), (1,)), ((), ())), p...  80 us
    all_gather x1, waiting for transfers between devices, local(): lax.all_gather(hidden, DP, axis=0, tiled=True)  74 us
    psum x1, waiting for transfers between devices, local(): out_full = lax.psum(out_part, 'tensor')  66.7 us
    psum x1, waiting for transfers between devices, local(): side = lax.psum(jnp.concatenate([a_in_part, a_out_part], axis=1), DP)  39 us
    dot_general x1, matrix products, local(): jnp.einsum('td,dkf->tkf', tokens, w_gate_up, preferred_element_type=jnp.f...  27.8 us
    reshape x1, local copies, waits for them, and re-layouts, local(): both = both.reshape(total, 2, n_core, width_h)  22.3 us
  transfers between devices with their start and end apart: 6, of which 6 were waited for; matrix products, arithmetic and copies ran while one was open for 3% of the time, Pallas kernels for 0%

profile of v4, /device:TPU:0, one launch (start us, length us, event | category | flops | bytes accessed | tf_op | source)
XLA Modules:
  0.0 661.9 jit_solution(11120823187496426604)
XLA Ops:
  6.5 0.0 copy-start
  6.5 0.0 all-reduce.9.cloned.1.call-start
  6.5 27.8 %fusion = f32[512,2,7168]{2,0,1:T(8,128)} fusion(bf16[1024,2,7168]{2,1,0:T(2,128)(2,1)} %param.8, bf16[512,1024]{1,0:T(8,128)(2,1)} %param.7), kind=kOutput, calls=%fused_computation.1 | convolution fusion | flops 15032385536 | bytes 59768832 | tf_op jit(solution)/shard_map/td,dkf->tkf/dot_general | solution.py:22
  34.4 22.3 %copy.39 = f32[2,64,2,8,3584]{4,3,1,2,0:T(8,128)} copy(f32[2,64,2,8,3584]{4,3,2,1,0:T(8,128)} %bitcast.74) | data formatting | bytes 58720256 | tf_op jit(solution)/shard_map/reshape | solution.py:23
  56.7 0.0 copy-start.4
  56.7 0.0 all-reduce.9.cloned.1.call-update
  56.7 0.0 reduce-scatter.6.cloned.1.call-start
  56.8 0.6 copy-done.4
  57.4 0.6 dynamic-slice
  57.9 93.2 %all-reduce.9.cloned.1.call-done = f32[512,2,2,3584]{3,0,2,1:T(8,128)} async-done(((f32[512,2,2,3584]{3,0,2,1:T(8,128)}), f32[512,2,2,3584]{3,0,2,1:T(8,128)}) %all-reduce.9.cloned.1.call-update) | async-done | bytes 29360144
  151.1 10.6 %fusion.3 = bf16[512,2,3584]{2,0,1:T(8,128)(2,1)} fusion(f32[512,2,2,3584]{3,0,2,1:T(8,128)} %all-reduce.9.cloned.1.call-done, u32[]{:T(128)} %bitcast.23, f32[]{:T(128)S(6)} %add.26), kind=kLoop, calls=%fused_computation.6 | loop fusion | flops 7340032 | bytes 22020104 | tf_op jit(solution)/shard_map/convert_element_type | solution.py:27
  161.7 0.0 reduce-scatter.6.cloned.1.call-update
  161.7 0.0 all-gather.2.cloned.1.call-start
  161.8 129.0 %reduce-scatter.6.cloned.1.call-done = bf16[128,2,3584]{2,0,1:T(8,128)(2,1)} async-done(((bf16[512,2,3584]{2,0,1:T(8,128)(2,1)}), bf16[128,2,3584]{2,0,1:T(8,128)(2,1)}) %reduce-scatter.6.cloned.1.call-update) | async-done | bytes 1835024 | tf_op jit(solution)/shard_map/reduce_scatter | solution.py:26
  290.8 3.4 copy.22
  294.2 6.7 %all_to_all.18 = f32[128,2,3584]{2,1,0:T(2,128)S(1)} all-to-all(f32[128,2,3584]{2,1,0:T(2,128)S(1)} %copy.22), channel_id=1, replica_groups=mesh['z'=4,'core'=2,'tensor'=4] {'core'}, dimensions={0} | all-to-all | bytes 7340032 | tf_op jit(solution)/shard_map/all_to_all | solution.py:29
  300.9 4.6 copy.40
  305.5 6.0 all_to_all.16
  311.6 3.5 multiply_convert_fusion
  315.0 0.0 all-gather.2.cloned.1.call-update
  315.1 0.0 copy-start.2
  315.1 0.0 all-reduce.5.cloned.1.call-start
  315.1 74.0 %all-gather.2.cloned.1.call-done = bf16[512,7168]{1,0:T(8,128)(2,1)} async-done(((bf16[64,7168]{1,0:T(8,128)(2,1)}), bf16[512,7168]{1,0:T(8,128)(2,1)}) %all-gather.2.cloned.1.call-update) | async-done | bytes 7340048 | tf_op jit(solution)/shard_map/all_gather | solution.py:36
  389.1 14.1 %fusion.41 = f32[512,1024]{1,0:T(8,128)} fusion(bf16[512,7168]{1,0:T(8,128)(2,1)} %all-gather.2.cloned.1.call-done, bf16[7168,1024]{1,0:T(8,128)(2,1)} %param.9), kind=kOutput, calls=%fused_computation.63 | convolution fusion | flops 7516192768 | bytes 24117248 | tf_op jit(solution)/shard_map/dot_general | solution.py:35
  403.2 0.0 all-reduce.5.cloned.1.call-update
  403.2 0.0 all-reduce.7.cloned.1.call-start
  403.3 0.0 copy-done.2
  403.3 1.7 fusion.32
  404.9 66.7 %all-reduce.5.cloned.1.call-done = f32[512,1024]{1,0:T(8,128)} async-done(((f32[512,1024]{1,0:T(8,128)}), f32[512,1024]{1,0:T(8,128)}) %all-reduce.5.cloned.1.call-update) | async-done | bytes 2097168 | tf_op jit(solution)/shard_map/psum | solution.py:38
  471.6 2.4 fusion.30
  474.0 0.7 pad_maximum_fusion
  474.7 0.0 all-reduce.7.cloned.1.call-update
  474.8 0.3 reduce-scatter.8.cloned.1.call-start
  475.0 13.9 %convolution_convert_fusion = bf16[512,7168]{1,0:T(8,128)(2,1)} fusion(bf16[7168,1024]{1,0:T(8,128)(2,1)} %param.9, f32[512,1024]{1,0:T(8,128)} %all-reduce.5.cloned.1.call-done, bf16[512,1024]{1,0:T(8,128)(2,1)} %param.10), kind=kOutput, calls=%fused_computation.5 | convolution fusion | flops 7521435648 | bytes 25165824 | tf_op jit(solution)/shard_map/dot_general | solution.py:43
  488.9 0.0 reduce-scatter.8.cloned.1.call-update
  489.0 1.8 fusion.15
  490.8 39.0 %all-reduce.7.cloned.1.call-done = f32[512,128]{0,1:T(8,128)} async-done(((f32[512,128]{0,1:T(8,128)}), f32[512,128]{0,1:T(8,128)}) %all-reduce.7.cloned.1.call-update) | async-done | bytes 262160 | tf_op jit(solution)/shard_map/psum | solution.py:41
  529.8 0.9 slice.50
  530.7 80.0 %reduce-scatter.8.cloned.1.call-done = bf16[64,7168]{1,0:T(8,128)(2,1)} async-done(((bf16[512,7168]{1,0:T(8,128)(2,1)}), bf16[64,7168]{1,0:T(8,128)(2,1)}) %reduce-scatter.8.cloned.1.call-update) | async-done | bytes 917520 | tf_op jit(solution)/shard_map/reduce_scatter | solution.py:42
  610.7 0.0 copy-start.1
  610.7 0.0 copy-start.3
  610.7 3.5 fusion.18
  614.2 0.1 copy-done.1
  614.4 0.2 copy-done.3
  614.6 1.9 fusion.13
  616.5 0.1 pad_maximum_fusion.2
  616.6 16.9 %psum.23 = f32[64,192]{1,0:T(8,128)S(1)} all-reduce(f32[64,192]{1,0:T(8,128)S(1)} %pad_maximum_fusion.2), channel_id=1, replica_groups=mesh['z'=4,'core'=2,'tensor'=4] {'tensor'}, use_global_device_ids=true, to_apply=%region_5.0 | all-reduce | flops 12288 | bytes 98304 | tf_op jit(solution)/shard_map/psum | solution.py:60
  633.4 14.8 %all_gather.7 = f32[512,192]{1,0:T(8,128)S(1)} all-gather(f32[64,192]{1,0:T(8,128)S(1)} %psum.23), channel_id=1, replica_groups=mesh['z'=4,'core'=2,'tensor'=4] {'z','core'}, dimensions={0}, use_global_device_ids=true | all-gather | bytes 442368 | tf_op jit(solution)/shard_map/all_gather | solution.py:60
  648.3 1.2 fusion.9
  649.5 1.3 fusion.10
  650.8 0.1 copy.26
  650.9 1.5 fusion.11
  652.4 0.9 pad_maximum_fusion.1
  653.3 0.2 convert_element_type.49
  653.5 0.0 copy-done
  653.5 1.5 fusion.42
  (4 shorter events, 0.0 us)
Async XLA Ops:
  6.5 647.0 %copy-start = (bf16[128,12288]{1,0:T(8,128)(2,1)S(1)}, bf16[128,12288]{1,0:T(8,128)(2,1)}, u32[]{:S(2)}) copy-start(bf16[128,12288]{1,0:T(8,128)(2,1)} %param.13) | copy-start | bytes 9437188
  6.5 144.6 %all-reduce.9.cloned.1.call-start = ((), (), s32[]{:S(2)}) async-start(), calls=%async_computation.8 | async-start | bytes 58720256
  56.7 0.7 copy-start.4
  56.7 234.1 %reduce-scatter.6.cloned.1.call-start = ((), (), s32[]{:S(2)}) async-start(), calls=%async_computation.3 | async-start | bytes 9175040 | tf_op jit(solution)/shard_map/reduce_scatter | solution.py:26
  161.7 227.4 %all-gather.2.cloned.1.call-start = ((), (), s32[]{:S(2)}) async-start(), calls=%async_computation.4 | async-start | bytes 8257536 | tf_op jit(solution)/shard_map/all_gather | solution.py:36
  315.1 88.2 %copy-start.2 = (bf16[1024,128]{1,0:T(8,128)(2,1)S(1)}, bf16[1024,128]{1,0:T(8,128)(2,1)}, u32[]{:S(2)}) copy-start(bf16[1024,128]{1,0:T(8,128)(2,1)} %param.11) | copy-start | bytes 786436
  315.1 156.6 %all-reduce.5.cloned.1.call-start = ((), (), s32[]{:S(2)}) async-start(), calls=%async_computation.5 | async-start | bytes 4194304 | tf_op jit(solution)/shard_map/psum | solution.py:38
  403.2 126.6 %all-reduce.7.cloned.1.call-start = ((), (), s32[]{:S(2)}) async-start(), calls=%async_computation.6 | async-start | bytes 524288 | tf_op jit(solution)/shard_map/psum | solution.py:41
  474.8 135.9 %reduce-scatter.8.cloned.1.call-start = ((), (), s32[]{:S(2)}) async-start(), calls=%async_computation.7 | async-start | bytes 8257536 | tf_op jit(solution)/shard_map/reduce_scatter | solution.py:42
  610.7 3.7 copy-start.1
  610.7 3.9 copy-start.3
Sparse Core Ops, SparseCore 0:
  56.9 94.2 all-reduce.8
  161.9 128.9 reduce-scatter.5
  315.2 73.8 all-gather.1
  403.3 68.2 all-reduce.4
  474.9 54.8 all-reduce.6
  531.9 78.6 reduce-scatter.7

commit v5 on v3

--- a/solution.py
+++ b/solution.py
@@ -12,16 +12,11 @@
     hi = lax.Precision.HIGHEST
     tests = total // SEQ
     a_in_part = jnp.dot(tokens, proj_model[:, :RANK], preferred_element_type=jnp.float32)
-    n_dp = lax.axis_size("dp")
-    rows = total // n_dp
-    width_ff = w_down.shape[0]
     both = jnp.einsum("td,dkf->ktf", tokens, w_gate_up, preferred_element_type=jnp.float32)
-    both = both.astype(jnp.bfloat16).reshape(2, n_dp, rows, width_ff).transpose(1, 0, 2, 3)
-    gate_up = lax.psum_scatter(
-        both.reshape(n_dp * 2 * rows, width_ff), "dp", scatter_dimension=0, tiled=True
-    ).astype(jnp.float32).reshape(2, rows, width_ff)
-    gate = gate_up[0]
-    up = gate_up[1]
+    gate = lax.psum_scatter(both[0], "dp", scatter_dimension=0, tiled=True)
+    up = lax.psum_scatter(
+        both[1].astype(jnp.bfloat16), "dp", scatter_dimension=0, tiled=True
+    ).astype(jnp.float32)
     sig = jax.nn.sigmoid(gate)
     act = gate * sig
     hidden = (act * up).astype(jnp.bfloat16)
@@ -35,11 +30,11 @@
     grad_hidden = lax.psum_scatter(
         lax.dot_general(
             cot, w_down, (((1,), (1,)), ((), ())), preferred_element_type=jnp.float32
-        ),
+        ).astype(jnp.bfloat16),
         "dp",
         scatter_dimension=0,
         tiled=True,
-    )
+    ).astype(jnp.float32)
     dgate = (grad_hidden * up * sig * (1.0 + gate * (1.0 - sig))).astype(jnp.bfloat16)
     dup = (grad_hidden * act).astype(jnp.bfloat16)
     hid_part = jnp.concatenate(

time: 617 us -> 647 us (1.049)
  local copies, waits for them, and re-layouts: 18.2 us -> 59.5 us
  waiting for transfers between devices: 477 us -> 460 us
    reduce_scatter x2 -> x0, waiting for transfers between devices: 301 us -> none  [the longest x1 152 us: local(): lax.psum_scatter(both.reshape(n_dp * 2 * rows, width_ff), 'dp', scatter_d...]
    unnamed x5 -> x9, waiting for transfers between devices: 0.08 us -> 283 us
    unnamed x10 -> x15, local copies, waits for them, and re-layouts: 3.4 us -> 34.1 us
    transpose x1 -> x0, local copies, waits for them, and re-layouts: 13.5 us -> none  [local(): both.astype(jnp.bfloat16).reshape(2, n_dp, rows, width_ff)]
    squeeze x0 -> x1, local copies, waits for them, and re-layouts: none -> 12.5 us  [local(): gate = lax.psum_scatter(both[0], 'dp', scatter_dimension=0, tiled=True)]
    convert_element_type x0 -> x2, local copies, waits for them, and re-layouts: none -> 11.7 us  [the longest x1 9.08 us: local(): both[1].astype(jnp.bfloat16)]
  transfers between devices with their start and end apart: 5 -> 6, of which waited for: 5 -> 6; matrix products, arithmetic and copies ran while one was open for 3% -> 7% of each run, Pallas kernels for 0% -> 0%
where the time goes in v5:
time: 647 us; the launch traced here: 646 us
  waiting for transfers between devices  460 us (71%)
  matrix products  74.5 us (12%)
  local copies, waits for them, and re-layouts  59.5 us (9%)
  blocking collectives  31.7 us (5%)
  between operations  13.6 us (2%)
  other arithmetic  6.55 us (1%)
    unnamed x9, waiting for transfers between devices  283 us
    all_gather x1, waiting for transfers between devices, local(): lax.all_gather(hidden, 'dp', axis=0, tiled=True)  71.8 us
    psum x1, waiting for transfers between devices, local(): out_full = lax.psum(out_part, 'tensor')  66.7 us
    psum x1, waiting for transfers between devices, local(): side = lax.psum(jnp.concatenate([a_in_part, a_out_part], axis=1), 'dp')  38.7 us
    unnamed x15, local copies, waits for them, and re-layouts  34.1 us
    dot_general x1, matrix products, local(): jnp.einsum('td,dkf->ktf', tokens, w_gate_up, preferred_element_type=jnp.f...  27.6 us
    psum x1, blocking collectives, local(): lax.psum(hid_part, 'tensor')  16.9 us
    all_gather x1, blocking collectives, local(): lax.all_gather(lax.psum(hid_part, 'tensor'), 'dp', axis=0, tiled=True)  14.8 us
  transfers between devices with their start and end apart: 6, of which 6 were waited for; matrix products, arithmetic and copies ran while one was open for 7% of the time, Pallas kernels for 0%

profile of v5, /device:TPU:0, one launch (start us, length us, event | category | flops | bytes accessed | tf_op | source)
XLA Modules:
  0.0 646.2 jit_solution(2107390434906719438)
XLA Ops:
  6.5 0.0 copy-start
  6.5 0.0 reduce-scatter.12.cloned.1.call-start
  6.5 27.6 %fusion.2 = f32[2,512,7168]{1,2,0:T(8,128)} fusion(bf16[1024,2,7168]{2,1,0:T(2,128)(2,1)} %param.8, bf16[512,1024]{1,0:T(8,128)(2,1)} %param.7), kind=kOutput, calls=%fused_computation.2 | convolution fusion | flops 15032385536 | bytes 59768832 | tf_op jit(solution)/shard_map/td,dkf->ktf/dot_general | solution.py:15
  34.2 9.1 %fusion.5 = bf16[512,7168]{0,1:T(8,128)(2,1)} fusion(f32[2,512,7168]{1,2,0:T(8,128)} %fusion.2), kind=kLoop, calls=%fused_computation.6 | loop fusion | bytes 14680064 | tf_op jit(solution)/shard_map/convert_element_type | solution.py:18
  43.2 10.1 %copy.32 = bf16[512,7168]{1,0:T(8,128)(2,1)} copy(bf16[512,7168]{0,1:T(8,128)(2,1)} %fusion.5) | data formatting | bytes 14680064
  53.3 0.0 reduce-scatter.12.cloned.1.call-update
  53.3 0.0 reduce-scatter.10.cloned.1.call-start
  53.4 12.5 %slice_bitcast_fusion = f32[512,7168]{0,1:T(8,128)} fusion(f32[2,512,7168]{1,2,0:T(8,128)} %fusion.2), kind=kLoop, calls=%fused_computation.4 | loop fusion | bytes 29360128 | tf_op jit(solution)/shard_map/squeeze | solution.py:16
  65.9 14.3 %copy.30 = f32[512,7168]{1,0:T(8,128)} copy(f32[512,7168]{0,1:T(8,128)} %slice_bitcast_fusion) | data formatting | bytes 29360128
  80.2 0.0 reduce-scatter.10.cloned.1.call-update
  80.2 0.2 all-gather.2.cloned.1.call-start
  80.4 55.5 %reduce-scatter.12.cloned.1.call-done = bf16[64,7168]{1,0:T(8,128)(2,1)} async-done(((bf16[512,7168]{1,0:T(8,128)(2,1)}), bf16[64,7168]{1,0:T(8,128)(2,1)}) %reduce-scatter.12.cloned.1.call-update) | async-done | bytes 917520
  135.9 2.6 copy.33
  138.5 147.1 %reduce-scatter.10.cloned.1.call-done = f32[64,7168]{1,0:T(8,128)} async-done(((f32[512,7168]{1,0:T(8,128)}), f32[64,7168]{1,0:T(8,128)}) %reduce-scatter.10.cloned.1.call-update) | async-done | bytes 1835024
  285.6 3.6 copy.31
  289.3 4.8 fusion.6
  294.1 2.6 copy.20
  296.6 0.0 all-gather.2.cloned.1.call-update
  296.7 0.0 copy-start.4
  296.7 0.0 all-reduce.3.cloned.1.call-start
  296.7 71.8 %all-gather.2.cloned.1.call-done = bf16[512,7168]{1,0:T(8,128)(2,1)} async-done(((bf16[64,7168]{1,0:T(8,128)(2,1)}), bf16[512,7168]{1,0:T(8,128)(2,1)}) %all-gather.2.cloned.1.call-update) | async-done | bytes 7340048 | tf_op jit(solution)/shard_map/all_gather | solution.py:24
  368.5 14.1 %fusion.44 = f32[512,1024]{1,0:T(8,128)} fusion(bf16[512,7168]{1,0:T(8,128)(2,1)} %all-gather.2.cloned.1.call-done, bf16[7168,1024]{1,0:T(8,128)(2,1)} %param.9), kind=kOutput, calls=%fused_computation.61 | convolution fusion | flops 7516192768 | bytes 24117248 | tf_op jit(solution)/shard_map/dot_general | solution.py:23
  382.6 0.0 all-reduce.3.cloned.1.call-update
  382.6 0.0 all-reduce.5.cloned.1.call-start
  382.7 0.0 copy-done.4
  382.7 1.7 fusion.36
  384.4 66.7 %all-reduce.3.cloned.1.call-done = f32[512,1024]{1,0:T(8,128)} async-done(((f32[512,1024]{1,0:T(8,128)}), f32[512,1024]{1,0:T(8,128)}) %all-reduce.3.cloned.1.call-update) | async-done | bytes 2097168 | tf_op jit(solution)/shard_map/psum | solution.py:26
  451.1 2.4 fusion.34
  453.4 0.7 pad_maximum_fusion
  454.2 0.0 all-reduce.5.cloned.1.call-update
  454.2 0.0 reduce-scatter.14.cloned.1.call-start
  454.2 13.9 %convolution_convert_fusion = bf16[512,7168]{1,0:T(8,128)(2,1)} fusion(bf16[7168,1024]{1,0:T(8,128)(2,1)} %param.9, f32[512,1024]{1,0:T(8,128)} %all-reduce.3.cloned.1.call-done, bf16[512,1024]{1,0:T(8,128)(2,1)} %param.10), kind=kOutput, calls=%fused_computation.5 | convolution fusion | flops 7521435648 | bytes 25165824 | tf_op jit(solution)/shard_map/dot_general | solution.py:31
  468.1 0.0 reduce-scatter.14.cloned.1.call-update
  468.2 2.4 fusion.20
  470.5 38.7 %all-reduce.5.cloned.1.call-done = f32[512,128]{0,1:T(8,128)} async-done(((f32[512,128]{0,1:T(8,128)}), f32[512,128]{0,1:T(8,128)}) %all-reduce.5.cloned.1.call-update) | async-done | bytes 262160 | tf_op jit(solution)/shard_map/psum | solution.py:29
  509.3 0.9 slice.51
  510.2 80.0 %reduce-scatter.14.cloned.1.call-done = bf16[64,7168]{1,0:T(8,128)(2,1)} async-done(((bf16[512,7168]{1,0:T(8,128)(2,1)}), bf16[64,7168]{1,0:T(8,128)(2,1)}) %reduce-scatter.14.cloned.1.call-update) | async-done | bytes 917520
  590.2 2.6 copy.35
  592.7 0.0 copy-start.1
  592.8 0.0 copy-start.2
  592.8 0.0 copy-start.3
  592.8 4.1 fusion.12
  596.9 0.0 copy-done.1
  596.9 0.4 copy-done.2
  597.3 0.5 copy-done.3
  597.8 2.9 fusion.14
  600.8 0.1 pad_maximum_fusion.2
  600.8 16.9 %psum.23 = f32[64,192]{1,0:T(8,128)S(1)} all-reduce(f32[64,192]{1,0:T(8,128)S(1)} %pad_maximum_fusion.2), channel_id=1, replica_groups=mesh['dp'=8,'tensor'=4] {'tensor'}, use_global_device_ids=true, to_apply=%region_5.0 | all-reduce | flops 12288 | bytes 98304 | tf_op jit(solution)/shard_map/psum | solution.py:48
  617.7 14.8 %all_gather.7 = f32[512,192]{1,0:T(8,128)S(1)} all-gather(f32[64,192]{1,0:T(8,128)S(1)} %psum.23), channel_id=1, replica_groups=mesh['dp'=8,'tensor'=4] {'dp'}, dimensions={0}, use_global_device_ids=true | all-gather | bytes 442368 | tf_op jit(solution)/shard_map/all_gather | solution.py:48
  632.6 1.3 fusion.17
  633.9 1.2 fusion.16
  635.1 0.1 copy.24
  635.2 1.5 fusion.18
  636.7 0.9 pad_maximum_fusion.1
  637.6 0.2 convert_element_type.42
  637.8 0.0 copy-done
  637.8 1.5 fusion.45
  (4 shorter events, 0.0 us)
Async XLA Ops:
  6.5 631.3 %copy-start = (bf16[128,12288]{1,0:T(8,128)(2,1)S(1)}, bf16[128,12288]{1,0:T(8,128)(2,1)}, u32[]{:S(2)}) copy-start(bf16[128,12288]{1,0:T(8,128)(2,1)} %param.13) | copy-start | bytes 9437188
  6.5 129.4 %reduce-scatter.12.cloned.1.call-start = ((), (), s32[]{:S(2)}) async-start(), calls=%async_computation.7 | async-start | bytes 8257536
  53.3 232.3 %reduce-scatter.10.cloned.1.call-start = ((), (), s32[]{:S(2)}) async-start(), calls=%async_computation.6 | async-start | bytes 16515072
  80.2 288.3 %all-gather.2.cloned.1.call-start = ((), (), s32[]{:S(2)}) async-start(), calls=%async_computation.3 | async-start | bytes 8257536 | tf_op jit(solution)/shard_map/all_gather | solution.py:24
  296.7 86.0 %copy-start.4 = (bf16[1024,128]{1,0:T(8,128)(2,1)S(1)}, bf16[1024,128]{1,0:T(8,128)(2,1)}, u32[]{:S(2)}) copy-start(bf16[1024,128]{1,0:T(8,128)(2,1)} %param.11) | copy-start | bytes 786436
  296.7 154.4 %all-reduce.3.cloned.1.call-start = ((), (), s32[]{:S(2)}) async-start(), calls=%async_computation.4 | async-start | bytes 4194304 | tf_op jit(solution)/shard_map/psum | solution.py:26
  382.6 126.6 %all-reduce.5.cloned.1.call-start = ((), (), s32[]{:S(2)}) async-start(), calls=%async_computation.5 | async-start | bytes 524288 | tf_op jit(solution)/shard_map/psum | solution.py:29
  454.2 136.0 %reduce-scatter.14.cloned.1.call-start = ((), (), s32[]{:S(2)}) async-start(), calls=%async_computation.8 | async-start | bytes 8257536
  592.7 4.1 copy-start.1
  592.8 4.5 copy-start.2
  592.8 5.1 copy-start.3
Sparse Core Ops, SparseCore 0:
  53.5 82.4 reduce-scatter.11
  138.2 147.3 reduce-scatter.9
  296.8 71.7 all-gather.1
  382.8 68.2 all-reduce.2
  454.3 54.9 all-reduce.4
  511.4 78.6 reduce-scatter.13
